TPU v7x, 512 devices: a whole 4x4x16 slice. The times are simulated.
512 devices in a mesh: ctx: 64 (over x, y, z_hi, core), head: 8 (over z_lo).
Axes of the slice: x: 4, y: 4, z: 16 (z_hi: 2, z_lo: 8; z = z_hi * 8 + z_lo), core: 2. Of those that a mesh axis runs over, the one named last changes fastest.
Arguments:
- query_head_rows: bfloat16 [16384, 4096], P('ctx', 'head'), may hold values from -4 to 4
- key_head_rows: bfloat16 [16384, 1024], P('ctx', 'head'), may hold values from -4 to 4
- value_head_rows: bfloat16 [16384, 1024], P('ctx', 'head'), may hold values from -4 to 4
- forward_output: bfloat16 [16384, 4096], P('ctx', 'head'), may hold values from -4 to 4, as said below
- cotangent: bfloat16 [16384, 4096], P('ctx', 'head'), may hold values from -6 to 6
- logsumexp: float32 [32, 16384], P('head', 'ctx'), as said below
- document_lengths: int32 [64], replicated, may hold values from 1 to 768, as said below
- linear_row_index: int32 [16384], replicated, may hold values from 0 to 16383, as said below
Outputs:
- query_gradient: bfloat16 [16384, 4096], P(('ctx', 'head'))
- linear_key_gradient: bfloat16 [16384, 1024], P(('ctx', 'head'))
- linear_value_gradient: bfloat16 [16384, 1024], P(('ctx', 'head'))
Inputs may be any that keep to these rules, and one draw needn't show every extreme that they name: `logsumexp`: for each head and position, the log of the sum of exp(scores) over the keys that the position sees, from the forward pass on these query_head_rows and key_head_rows. `forward_output`: for each head, the forward pass's softmax weights times value_head_rows, rounded to bfloat16. `document_lengths`: the lengths sum to 16384; the longest document has exactly 768 tokens. `linear_row_index`: A permutation of the 16384 positions. Counting positions in blocks of 256, from one block of the packed sequence at most 8 rows go to one block of linear positions, some pair of blocks reaches 8, and every linear block receives 256 rows.
All inputs are finite; a program needn't handle non-finite values.
Results may differ from a plain program's by a relative error of at most 0.0049.
Values may be sent and summed in bfloat16 or wider, within the bound.
No kernel may reach another device: no remote copies, remote signals or barrier semaphores. Data moves between devices by JAX's collectives and lax.ppermute only.
A program may use at most 64 MiB of HBM per device.

v0:
```python
import jax
import jax.numpy as jnp
from jax import lax
from jax.sharding import PartitionSpec as P

HEAD_SIZE = 128
DOC_BLOCKS = 3


def from_behind(shard, axis, by):
    count = lax.axis_size(axis)
    pairs = [(i, i + by) for i in range(count) if 0 <= i + by < count]
    return lax.ppermute(shard, axis, pairs)


def shifted(block, axis, distance):
    devices = range(lax.axis_size(axis))
    route = [((i - distance) % len(devices), i) for i in devices]
    return lax.ppermute(block, axis, route)


def block_grads(
    query_vectors,
    output_gradient,
    log_normalizer,
    row_correction,
    begins,
    query_pos,
    key_part,
    value_part,
    key_start,
):
    length = query_vectors.shape[0]
    kv_heads = query_vectors.shape[1]
    scaling = HEAD_SIZE ** (-0.5)
    key_heads = key_part.reshape(length, kv_heads, HEAD_SIZE)
    value_heads = value_part.reshape(length, kv_heads, HEAD_SIZE)
    scores = (
        jnp.einsum("qngd,knd->qngk", query_vectors, key_heads, preferred_element_type=jnp.float32)
        * scaling
    )
    key_pos = key_start + lax.iota(jnp.int32, length)
    visible = (key_pos[None, :] <= query_pos[:, None]) & (key_pos[None, :] >= begins[:, None])
    weights = jnp.exp(
        jnp.where(visible[:, None, None, :], scores - log_normalizer[..., None], -jnp.inf)
    )
    weights_low = weights.astype(jnp.bfloat16)
    grad_weights = jnp.einsum(
        "qngd,knd->qngk", output_gradient, value_heads, preferred_element_type=jnp.float32
    )
    grad_scores = (weights * (grad_weights - row_correction[..., None]) * scaling).astype(
        jnp.bfloat16
    )
    query_term = jnp.einsum(
        "qngk,knd->qngd", grad_scores, key_heads, preferred_element_type=jnp.float32
    )
    key_term = jnp.einsum(
        "qngk,qngd->knd", grad_scores, query_vectors, preferred_element_type=jnp.float32
    )
    value_term = jnp.einsum(
        "qngk,qngd->knd", weights_low, output_gradient, preferred_element_type=jnp.float32
    )
    return (query_term, key_term.reshape(length, -1), value_term.reshape(length, -1))


def per_device(
    query_head_rows,
    key_head_rows,
    value_head_rows,
    forward_output,
    cotangent,
    logsumexp,
    document_lengths,
    linear_row_index,
):
    length = query_head_rows.shape[0]
    kv_heads = key_head_rows.shape[1] // HEAD_SIZE
    query_groups = logsumexp.shape[0] // kv_heads
    block_index = lax.axis_index("ctx")
    blocks = lax.axis_size("ctx")
    query_pos = block_index * length + lax.iota(jnp.int32, length)
    finish = jnp.cumsum(document_lengths)
    firsts = finish - document_lengths
    begins = jnp.max(jnp.where(firsts[None, :] <= query_pos[:, None], firsts[None, :], 0), axis=1)
    query_vectors = query_head_rows.reshape(length, kv_heads, query_groups, HEAD_SIZE)
    output_gradient = cotangent.reshape(length, kv_heads, query_groups, HEAD_SIZE)
    log_normalizer = logsumexp.T.reshape(length, kv_heads, query_groups)
    row_correction = jnp.sum(
        output_gradient.astype(jnp.float32)
        * forward_output.reshape(length, kv_heads, query_groups, HEAD_SIZE).astype(jnp.float32),
        axis=3,
    )

    def block_terms(key_part, value_part, distance):
        key_start = (block_index - distance) * length
        return block_grads(
            query_vectors,
            output_gradient,
            log_normalizer,
            row_correction,
            begins,
            query_pos,
            key_part,
            value_part,
            key_start,
        )

    query_acc, key_running_sum, value_running_sum = block_terms(key_head_rows, value_head_rows, 0)
    moving_keys, moving_values = (key_head_rows, value_head_rows)
    for distance in range(1, DOC_BLOCKS + 1):
        moving_keys, moving_values = from_behind((moving_keys, moving_values), "ctx", 1)
        key_running_sum, value_running_sum = shifted((key_running_sum, value_running_sum), "ctx", 1)
        query_term, key_term, value_term = block_terms(moving_keys, moving_values, distance)
        query_acc = query_acc + query_term
        key_running_sum = key_running_sum + key_term
        value_running_sum = value_running_sum + value_term
    key_running_sum, value_running_sum = (
        shifted(key_running_sum.astype(jnp.bfloat16), "ctx", -DOC_BLOCKS).astype(
            key_running_sum.dtype
        ),
        shifted(value_running_sum.astype(jnp.bfloat16), "ctx", -DOC_BLOCKS).astype(
            value_running_sum.dtype
        ),
    )
    query_grad = query_acc.reshape(length, -1).astype(jnp.bfloat16)
    key_row_gradient = key_running_sum.astype(jnp.bfloat16)
    value_row_gradient = value_running_sum.astype(jnp.bfloat16)
    capacity = 2 * length // blocks
    own_targets = lax.dynamic_slice_in_dim(linear_row_index, block_index * length, length)
    target = own_targets // length
    owner_marks = (target[:, None] == lax.iota(jnp.int32, blocks)[None, :]).astype(jnp.int32)
    slot_rank = jnp.sum(owner_marks * (jnp.cumsum(owner_marks, axis=0) - 1), axis=1)
    send_slots = target * capacity + slot_rank

    def pack_slots(grad_rows):
        return (
            jnp.zeros((blocks * capacity, grad_rows.shape[1]), grad_rows.dtype)
            .at[send_slots]
            .set(grad_rows)
        )

    arrived = (
        lax.all_to_all(pack_slots(query_grad), "ctx", split_axis=0, concat_axis=0, tiled=True),
        lax.all_to_all(
            pack_slots(key_row_gradient), "ctx", split_axis=0, concat_axis=0, tiled=True
        ),
        lax.all_to_all(
            pack_slots(value_row_gradient), "ctx", split_axis=0, concat_axis=0, tiled=True
        ),
    )
    all_owners = linear_row_index.reshape(blocks, length)
    landing = all_owners // length == block_index
    landed_rank = jnp.cumsum(landing.astype(jnp.int32), axis=1) - 1
    source_slot = lax.iota(jnp.int32, blocks)[:, None] * capacity + landed_rank
    where_to = jnp.where(landing, all_owners % length, length)
    inverse = (
        jnp.zeros((length,), jnp.int32)
        .at[where_to.reshape(-1)]
        .set(source_slot.reshape(-1), mode="drop")
    )
    linear_query = arrived[0][inverse]
    linear_key = arrived[1][inverse]
    linear_value = arrived[2][inverse]
    result = (
        lax.all_to_all(linear_query, "head", split_axis=0, concat_axis=1, tiled=True),
        lax.all_to_all(linear_key, "head", split_axis=0, concat_axis=1, tiled=True),
        lax.all_to_all(linear_value, "head", split_axis=0, concat_axis=1, tiled=True),
    )
    return (result[0], result[1], result[2])


def solution(mesh):
    placed = (
        P("ctx", "head"),
        P("ctx", "head"),
        P("ctx", "head"),
        P("ctx", "head"),
        P("ctx", "head"),
        P("head", "ctx"),
        P(),
        P(),
    )
    return jax.shard_map(
        per_device,
        mesh=mesh,
        in_specs=placed,
        out_specs=(P(("ctx", "head"), None), P(("ctx", "head"), None), P(("ctx", "head"), None)),
        check_vma=False,
    )
```

profile of v0, /device:TPU:32, one launch (start us, length us, event | category | flops | bytes accessed | tf_op | source)
XLA Modules:
  0.0 360.1 jit_solution(3413833666730126142)
XLA Ops:
  0.6 1.9 collective-permute-start.1
  2.5 15.1 %collective-permute-start = (bf16[256,128]{1,0:T(8,128)(2,1)}, bf16[256,128]{1,0:T(8,128)(2,1)S(1)}, u32[]{:S(2)}, u32[]{:S(2)}) collective-permute-start(bf16[256,128]{1,0:T(8,128)(2,1)} %param.9), channel_id=1, source_target_pairs={{0,8},{8,16},{16,24},{24,32},{32,40},{40,48},{48,56},{56,64},{64,7... | collective-permute-start | bytes 196616 | tf_op jit(solution)/shard_map/ppermute | solution.py:13
  17.7 0.6 copy-done.14
  18.6 1.1 convert_multiply_fusion
  19.9 0.3 reduce_sum.19
  20.8 0.5 copy-done.6
  21.3 0.4 fusion.23
  21.7 0.6 copy-done.1
  22.3 0.3 fusion.40
  22.6 0.3 convolution_bitcast_fusion.11
  22.9 2.1 collective-permute-start.6
  24.9 0.3 convolution_bitcast_fusion.7
  25.2 1.9 collective-permute-start.10
  27.4 1.1 fusion.89
  28.5 0.6 reduce-window.24
  29.7 0.6 reduce-window.32
  30.7 60.3 %scatter_custom_fusion.1 = s32[256]{0:T(256)S(1)} fusion(s32[16384]{0:T(1024)S(1)} %compare_select_fusion, s32[16384]{0:T(1024)S(1)} %add.156, s32[]{:T(128)} %constant.73.clone.1), kind=kCustom, calls=%fused_computation.185 | custom fusion | bytes 1028 | tf_op jit(solution)/shard_map/scatter | solution.py:159
  91.0 1.9 collective-permute-start.3
  93.0 13.9 %collective-permute-start.2 = (bf16[256,128]{1,0:T(8,128)(2,1)S(1)}, bf16[256,128]{1,0:T(8,128)(2,1)S(1)}, u32[]{:S(2)}, u32[]{:S(2)}) collective-permute-start(bf16[256,128]{1,0:T(8,128)(2,1)S(1)} %collective-permute-done), channel_id=1, source_target_pairs={{0,8},{8,16},{16,24},{24,32},{32,40},{40,48},{48,56},{56,64},{64,7... | collective-permute-start | bytes 196616 | tf_op jit(solution)/shard_map/ppermute | solution.py:13
  106.9 0.4 fusion.27
  107.3 0.3 fusion.41
  107.8 2.3 collective-permute-start.4
  110.1 0.4 fusion.31
  110.5 0.3 fusion.42
  110.8 0.3 fusion.45
  111.1 0.3 convolution_bitcast_fusion.9
  111.4 16.5 %collective-permute-start.7 = (f32[256,128]{1,0:T(8,128)S(1)}, f32[256,128]{1,0:T(8,128)S(1)}, u32[]{:S(2)}, u32[]{:S(2)}) collective-permute-start(f32[256,128]{1,0:T(8,128)S(1)} %fusion.45), channel_id=1, source_target_pairs={{504,0},{0,8},{8,16},{16,24},{24,32},{32,40},{40,48},{48,56},{56,6... | collective-permute-start | bytes 393224 | tf_op jit(solution)/shard_map/ppermute | solution.py:19
  127.9 1.9 collective-permute-start.5
  129.8 0.4 fusion.35
  130.7 0.3 fusion.43
  131.0 4.1 %collective-permute-done.7 = f32[256,128]{1,0:T(8,128)S(1)} collective-permute-done((f32[256,128]{1,0:T(8,128)S(1)}, f32[256,128]{1,0:T(8,128)S(1)}, u32[]{:S(2)}, u32[]{:S(2)}) %collective-permute-start.7) | collective-permute-done | bytes 131104 | tf_op jit(solution)/shard_map/ppermute | solution.py:19
  135.1 1.9 collective-permute-start.8
  137.1 0.3 convolution_bitcast_fusion.8
  137.4 18.8 %collective-permute-done.8 = f32[256,128]{1,0:T(8,128)S(1)} collective-permute-done((f32[256,128]{1,0:T(8,128)S(1)}, f32[256,128]{1,0:T(8,128)S(1)}, u32[]{:S(2)}, u32[]{:S(2)}) %collective-permute-start.8) | collective-permute-done | bytes 131104 | tf_op jit(solution)/shard_map/ppermute | solution.py:19
  156.2 1.9 collective-permute-start.9
  158.2 0.3 fusion.46
  158.4 12.3 %collective-permute-start.11 = (f32[256,128]{1,0:T(8,128)S(1)}, f32[256,128]{1,0:T(8,128)S(1)}, u32[]{:S(2)}, u32[]{:S(2)}) collective-permute-start(f32[256,128]{1,0:T(8,128)S(1)} %fusion.46), channel_id=1, source_target_pairs={{504,0},{0,8},{8,16},{16,24},{24,32},{32,40},{40,48},{48,56},{56,6... | collective-permute-start | bytes 393224 | tf_op jit(solution)/shard_map/ppermute | solution.py:19
  170.8 2.1 scatter_custom_fusion.2
  172.8 21.6 %all-to-all-start.2 = ((bf16[64,8,128]{2,1,0:T(8,128)(2,1)}), bf16[64,8,128]{2,1,0:T(8,128)(2,1)S(1)}, u32[]{:S(2)}, u32[]{:S(2)}) async-start(bf16[64,8,128]{2,1,0:T(8,128)(2,1)} %bitcast.50), calls=%async_computation.2 | async-start | bytes 262144 | tf_op jit(solution)/shard_map/all_to_all | solution.py:144
  194.4 0.3 convolution_bitcast_fusion.5
  194.8 2.0 collective-permute-start.12
  196.7 0.3 convolution_bitcast_fusion.4
  197.0 21.8 %collective-permute-done.12 = f32[256,128]{1,0:T(8,128)S(1)} collective-permute-done((f32[256,128]{1,0:T(8,128)S(1)}, f32[256,128]{1,0:T(8,128)S(1)}, u32[]{:S(2)}, u32[]{:S(2)}) %collective-permute-start.12) | collective-permute-done | bytes 131104 | tf_op jit(solution)/shard_map/ppermute | solution.py:19
  218.9 1.9 collective-permute-start.13
  220.8 12.4 %collective-permute-done.13 = bf16[256,128]{1,0:T(8,128)(2,1)S(1)} collective-permute-done((bf16[256,128]{1,0:T(8,128)(2,1)S(1)}, bf16[256,128]{1,0:T(8,128)(2,1)S(1)}, u32[]{:S(2)}, u32[]{:S(2)}) %collective-permute-start.13) | collective-permute-done | bytes 65568 | tf_op jit(solution)/shard_map/ppermute | solution.py:19
  233.2 1.8 scatter_custom_fusion.3
  235.0 15.5 %all-to-all-start.4 = ((bf16[64,8,128]{2,1,0:T(8,128)(2,1)}), bf16[64,8,128]{2,1,0:T(8,128)(2,1)S(1)}, u32[]{:S(2)}, u32[]{:S(2)}) async-start(bf16[64,8,128]{2,1,0:T(8,128)(2,1)} %bitcast.62), calls=%async_computation.4 | async-start | bytes 262144 | tf_op jit(solution)/shard_map/all_to_all | solution.py:147
  250.8 0.6 copy-done.10
  251.7 1.5 gather_fusion.1
  253.1 16.4 %all-to-all-done.4 = bf16[64,8,128]{2,1,0:T(8,128)(2,1)S(1)} async-done(((bf16[64,8,128]{2,1,0:T(8,128)(2,1)}), bf16[64,8,128]{2,1,0:T(8,128)(2,1)S(1)}, u32[]{:S(2)}, u32[]{:S(2)}) %all-to-all-start.4) | async-done | bytes 131104 | tf_op jit(solution)/shard_map/all_to_all | solution.py:147
  269.5 4.7 %all-to-all-start.3 = ((bf16[8,32,128]{2,1,0:T(8,128)(2,1)}), bf16[8,32,128]{2,1,0:T(8,128)(2,1)S(1)}, u32[]{:S(2)}, u32[]{:S(2)}) async-start(bf16[8,32,128]{2,1,0:T(8,128)(2,1)} %bitcast.52), calls=%async_computation.3 | async-start | bytes 131072 | tf_op jit(solution)/shard_map/all_to_all | solution.py:166
  274.6 2.3 scatter_custom_fusion
  276.9 6.5 %all-to-all-done.3 = bf16[8,32,128]{2,1,0:T(8,128)(2,1)S(1)} async-done(((bf16[8,32,128]{2,1,0:T(8,128)(2,1)}), bf16[8,32,128]{2,1,0:T(8,128)(2,1)S(1)}, u32[]{:S(2)}, u32[]{:S(2)}) %all-to-all-start.3) | async-done | bytes 65568 | tf_op jit(solution)/shard_map/all_to_all | solution.py:166
  283.5 4.6 %all-to-all-start = ((bf16[64,8,512]{2,1,0:T(8,128)(2,1)}), bf16[64,8,512]{2,1,0:T(8,128)(2,1)S(1)}, u32[]{:S(2)}, u32[]{:S(2)}) async-start(bf16[64,8,512]{2,1,0:T(8,128)(2,1)} %bitcast.40), calls=%async_computation | async-start | bytes 1048576 | tf_op jit(solution)/shard_map/all_to_all | solution.py:143
  288.1 1.5 gather_fusion.2
  289.6 36.7 %all-to-all-done = bf16[64,8,512]{2,1,0:T(8,128)(2,1)S(1)} async-done(((bf16[64,8,512]{2,1,0:T(8,128)(2,1)}), bf16[64,8,512]{2,1,0:T(8,128)(2,1)S(1)}, u32[]{:S(2)}, u32[]{:S(2)}) %all-to-all-start) | async-done | bytes 524320 | tf_op jit(solution)/shard_map/all_to_all | solution.py:143
  326.3 3.3 all-to-all-start.5
  329.6 1.9 gather_fusion
  331.4 7.4 %all-to-all-done.5 = bf16[8,32,128]{2,1,0:T(8,128)(2,1)S(1)} async-done(((bf16[8,32,128]{2,1,0:T(8,128)(2,1)}), bf16[8,32,128]{2,1,0:T(8,128)(2,1)S(1)}, u32[]{:S(2)}, u32[]{:S(2)}) %all-to-all-start.5) | async-done | bytes 65568 | tf_op jit(solution)/shard_map/all_to_all | solution.py:167
  338.8 5.0 %all-to-all-start.1 = ((bf16[8,32,512]{2,1,0:T(8,128)(2,1)}), bf16[8,32,512]{2,1,0:T(8,128)(2,1)S(1)}, u32[]{:S(2)}, u32[]{:S(2)}) async-start(bf16[8,32,512]{2,1,0:T(8,128)(2,1)} %bitcast.44), calls=%async_computation.1 | async-start | bytes 524288 | tf_op jit(solution)/shard_map/all_to_all | solution.py:165
  343.8 0.6 copy_bitcast_fusion.1
  344.4 0.6 copy_bitcast_fusion
  345.1 14.3 %all-to-all-done.1 = bf16[8,32,512]{2,1,0:T(8,128)(2,1)S(1)} async-done(((bf16[8,32,512]{2,1,0:T(8,128)(2,1)}), bf16[8,32,512]{2,1,0:T(8,128)(2,1)S(1)}, u32[]{:S(2)}, u32[]{:S(2)}) %all-to-all-start.1) | async-done | bytes 262176 | tf_op jit(solution)/shard_map/all_to_all | solution.py:165
  359.4 0.7 copy.125
  (78 shorter events, 3.9 us)
Async XLA Ops:
  0.6 20.1 %copy-start = (bf16[256,512]{1,0:T(8,128)(2,1)S(1)}, bf16[256,512]{1,0:T(8,128)(2,1)}, u32[]{:S(2)}) copy-start(bf16[256,512]{1,0:T(8,128)(2,1)} %param.8) | copy-start | bytes 786436
  0.6 90.4 %collective-permute-start.1 = (bf16[256,128]{1,0:T(8,128)(2,1)}, bf16[256,128]{1,0:T(8,128)(2,1)S(1)}, u32[]{:S(2)}, u32[]{:S(2)}) collective-permute-start(bf16[256,128]{1,0:T(8,128)(2,1)} %param.10), channel_id=1, source_target_pairs={{0,8},{8,16},{16,24},{24,32},{32,40},{40,48},{48,56},{56,64},{64,7... | collective-permute-start | bytes 196616 | tf_op jit(solution)/shard_map/ppermute | solution.py:13
  2.5 90.5 %collective-permute-start = (bf16[256,128]{1,0:T(8,128)(2,1)}, bf16[256,128]{1,0:T(8,128)(2,1)S(1)}, u32[]{:S(2)}, u32[]{:S(2)}) collective-permute-start(bf16[256,128]{1,0:T(8,128)(2,1)} %param.9), channel_id=1, source_target_pairs={{0,8},{8,16},{16,24},{24,32},{32,40},{40,48},{48,56},{56,64},{64,7... | collective-permute-start | bytes 196616 | tf_op jit(solution)/shard_map/ppermute | solution.py:13
  17.7 0.7 copy-start.14
  20.5 0.8 copy-start.6
  20.5 0.8 copy-start.15
  21.3 1.0 copy-start.1
  21.3 1.0 copy-start.13
  22.9 4.3 %copy-start.5 = (s32[16384]{0:T(1024)S(1)}, s32[16384]{0:T(1024)}, u32[]{:S(2)}) copy-start(s32[16384]{0:T(1024)} %param.15) | copy-start | bytes 196612
  22.9 88.0 %collective-permute-start.6 = (f32[256,128]{1,0:T(8,128)S(1)}, f32[256,128]{1,0:T(8,128)S(1)}, u32[]{:S(2)}, u32[]{:S(2)}) collective-permute-start(f32[256,128]{1,0:T(8,128)S(1)} %convolution_bitcast_fusion.11), channel_id=1, source_target_pairs={{504,0},{0,8},{8,16},{16,24},{24,32},{32,40},{40,48},{48,56},{56,6... | collective-permute-start | bytes 393224 | tf_op jit(solution)/shard_map/ppermute | solution.py:19
  25.2 132.9 %collective-permute-start.10 = (f32[256,128]{1,0:T(8,128)S(1)}, f32[256,128]{1,0:T(8,128)S(1)}, u32[]{:S(2)}, u32[]{:S(2)}) collective-permute-start(f32[256,128]{1,0:T(8,128)S(1)} %convolution_bitcast_fusion.7), channel_id=1, source_target_pairs={{504,0},{0,8},{8,16},{16,24},{24,32},{32,40},{40,48},{48,56},{56,6... | collective-permute-start | bytes 393224 | tf_op jit(solution)/shard_map/ppermute | solution.py:19
  91.0 19.5 %collective-permute-start.3 = (bf16[256,128]{1,0:T(8,128)(2,1)S(1)}, bf16[256,128]{1,0:T(8,128)(2,1)S(1)}, u32[]{:S(2)}, u32[]{:S(2)}) collective-permute-start(bf16[256,128]{1,0:T(8,128)(2,1)S(1)} %collective-permute-done.1), channel_id=1, source_target_pairs={{0,8},{8,16},{16,24},{24,32},{32,40},{40,48},{48,56},{56,64},{64,7... | collective-permute-start | bytes 196616 | tf_op jit(solution)/shard_map/ppermute | solution.py:13
  93.0 14.3 %copy-start.7 = (bf16[256,128]{1,0:T(8,128)(2,1)}, bf16[256,128]{1,0:T(8,128)(2,1)S(1)}, u32[]{:S(2)}) copy-start(bf16[256,128]{1,0:T(8,128)(2,1)S(1)} %collective-permute-done) | copy-start | bytes 196612
  93.0 14.8 %collective-permute-start.2 = (bf16[256,128]{1,0:T(8,128)(2,1)S(1)}, bf16[256,128]{1,0:T(8,128)(2,1)S(1)}, u32[]{:S(2)}, u32[]{:S(2)}) collective-permute-start(bf16[256,128]{1,0:T(8,128)(2,1)S(1)} %collective-permute-done), channel_id=1, source_target_pairs={{0,8},{8,16},{16,24},{24,32},{32,40},{40,48},{48,56},{56,64},{64,7... | collective-permute-start | bytes 196616 | tf_op jit(solution)/shard_map/ppermute | solution.py:13
  107.8 2.7 copy-start.9
  107.8 22.1 %collective-permute-start.4 = (bf16[256,128]{1,0:T(8,128)(2,1)S(1)}, bf16[256,128]{1,0:T(8,128)(2,1)S(1)}, u32[]{:S(2)}, u32[]{:S(2)}) collective-permute-start(bf16[256,128]{1,0:T(8,128)(2,1)S(1)} %collective-permute-done.2), channel_id=1, source_target_pairs={{0,8},{8,16},{16,24},{24,32},{32,40},{40,48},{48,56},{56,64},{64,7... | collective-permute-start | bytes 196616 | tf_op jit(solution)/shard_map/ppermute | solution.py:13
  111.4 23.7 %collective-permute-start.7 = (f32[256,128]{1,0:T(8,128)S(1)}, f32[256,128]{1,0:T(8,128)S(1)}, u32[]{:S(2)}, u32[]{:S(2)}) collective-permute-start(f32[256,128]{1,0:T(8,128)S(1)} %fusion.45), channel_id=1, source_target_pairs={{504,0},{0,8},{8,16},{16,24},{24,32},{32,40},{40,48},{48,56},{56,6... | collective-permute-start | bytes 393224 | tf_op jit(solution)/shard_map/ppermute | solution.py:19
  127.9 2.8 collective-permute-start.5
  129.8 0.6 copy-start.11
  130.4 4.7 %copy-start.2 = (f32[256,1,4,256]{0,3,2,1:T(8,128)}, f32[256,1,4,256]{0,3,2,1:T(8,128)S(1)}, u32[]{:S(2)}) copy-start(f32[256,1,4,256]{0,3,2,1:T(8,128)S(1)} %fusion.35) | copy-start | bytes 3145732
  135.1 21.0 %collective-permute-start.8 = (f32[256,128]{1,0:T(8,128)S(1)}, f32[256,128]{1,0:T(8,128)S(1)}, u32[]{:S(2)}, u32[]{:S(2)}) collective-permute-start(f32[256,128]{1,0:T(8,128)S(1)} %add.159), channel_id=1, source_target_pairs={{504,0},{0,8},{8,16},{16,24},{24,32},{32,40},{40,48},{48,56},{56,6... | collective-permute-start | bytes 393224 | tf_op jit(solution)/shard_map/ppermute | solution.py:19
  156.2 14.5 %collective-permute-start.9 = (bf16[256,128]{1,0:T(8,128)(2,1)S(1)}, bf16[256,128]{1,0:T(8,128)(2,1)}, u32[]{:S(2)}, u32[]{:S(2)}) collective-permute-start(bf16[256,128]{1,0:T(8,128)(2,1)S(1)} %add_convert_fusion.1), channel_id=1, source_target_pairs={{24,0},{32,8},{40,16},{48,24},{56,32},{64,40},{72,48},{80,56},{88,... | collective-permute-start | bytes 196616 | tf_op jit(solution)/shard_map/ppermute | solution.py:19
  158.4 36.3 %collective-permute-start.11 = (f32[256,128]{1,0:T(8,128)S(1)}, f32[256,128]{1,0:T(8,128)S(1)}, u32[]{:S(2)}, u32[]{:S(2)}) collective-permute-start(f32[256,128]{1,0:T(8,128)S(1)} %fusion.46), channel_id=1, source_target_pairs={{504,0},{0,8},{8,16},{16,24},{24,32},{32,40},{40,48},{48,56},{56,6... | collective-permute-start | bytes 393224 | tf_op jit(solution)/shard_map/ppermute | solution.py:19
  172.8 62.1 %all-to-all-start.2 = ((bf16[64,8,128]{2,1,0:T(8,128)(2,1)}), bf16[64,8,128]{2,1,0:T(8,128)(2,1)S(1)}, u32[]{:S(2)}, u32[]{:S(2)}) async-start(bf16[64,8,128]{2,1,0:T(8,128)(2,1)} %bitcast.50), calls=%async_computation.2 | async-start | bytes 262144 | tf_op jit(solution)/shard_map/all_to_all | solution.py:144
  194.4 2.3 copy-start.3
  194.8 24.1 %collective-permute-start.12 = (f32[256,128]{1,0:T(8,128)S(1)}, f32[256,128]{1,0:T(8,128)S(1)}, u32[]{:S(2)}, u32[]{:S(2)}) collective-permute-start(f32[256,128]{1,0:T(8,128)S(1)} %add.162), channel_id=1, source_target_pairs={{504,0},{0,8},{8,16},{16,24},{24,32},{32,40},{40,48},{48,56},{56,6... | collective-permute-start | bytes 393224 | tf_op jit(solution)/shard_map/ppermute | solution.py:19
  197.0 53.5 %copy-start.4 = (f32[256,4,128]{0,2,1:T(8,128)S(1)}, f32[256,4,128]{0,2,1:T(8,128)}, u32[]{:S(2)}) copy-start(f32[256,4,128]{0,2,1:T(8,128)} %fusion.89) | copy-start | bytes 1572868
  218.9 14.3 %collective-permute-start.13 = (bf16[256,128]{1,0:T(8,128)(2,1)S(1)}, bf16[256,128]{1,0:T(8,128)(2,1)S(1)}, u32[]{:S(2)}, u32[]{:S(2)}) collective-permute-start(bf16[256,128]{1,0:T(8,128)(2,1)S(1)} %add_convert_fusion), channel_id=1, source_target_pairs={{24,0},{32,8},{40,16},{48,24},{56,32},{64,40},{72,48},{80,56},{88,... | collective-permute-start | bytes 196616 | tf_op jit(solution)/shard_map/ppermute | solution.py:19
  235.0 15.6 %copy-start.8 = (bf16[256,128]{1,0:T(8,128)(2,1)S(1)}, bf16[256,128]{1,0:T(8,128)(2,1)}, u32[]{:S(2)}) copy-start(bf16[256,128]{1,0:T(8,128)(2,1)} %copy-done.7) | copy-start | bytes 196612
  235.0 34.5 %all-to-all-start.4 = ((bf16[64,8,128]{2,1,0:T(8,128)(2,1)}), bf16[64,8,128]{2,1,0:T(8,128)(2,1)S(1)}, u32[]{:S(2)}, u32[]{:S(2)}) async-start(bf16[64,8,128]{2,1,0:T(8,128)(2,1)} %bitcast.62), calls=%async_computation.4 | async-start | bytes 262144 | tf_op jit(solution)/shard_map/all_to_all | solution.py:147
  250.5 0.8 copy-start.10
  269.5 4.7 %copy-start.12 = (bf16[256,128]{1,0:T(8,128)(2,1)S(1)}, bf16[256,128]{1,0:T(8,128)(2,1)}, u32[]{:S(2)}) copy-start(bf16[256,128]{1,0:T(8,128)(2,1)} %copy-done.11) | copy-start | bytes 196612
  269.5 13.9 %all-to-all-start.3 = ((bf16[8,32,128]{2,1,0:T(8,128)(2,1)}), bf16[8,32,128]{2,1,0:T(8,128)(2,1)S(1)}, u32[]{:S(2)}, u32[]{:S(2)}) async-start(bf16[8,32,128]{2,1,0:T(8,128)(2,1)} %bitcast.52), calls=%async_computation.3 | async-start | bytes 131072 | tf_op jit(solution)/shard_map/all_to_all | solution.py:166
  283.5 42.8 %all-to-all-start = ((bf16[64,8,512]{2,1,0:T(8,128)(2,1)}), bf16[64,8,512]{2,1,0:T(8,128)(2,1)S(1)}, u32[]{:S(2)}, u32[]{:S(2)}) async-start(bf16[64,8,512]{2,1,0:T(8,128)(2,1)} %bitcast.40), calls=%async_computation | async-start | bytes 1048576 | tf_op jit(solution)/shard_map/all_to_all | solution.py:143
  326.3 12.6 %all-to-all-start.5 = ((bf16[8,32,128]{2,1,0:T(8,128)(2,1)}), bf16[8,32,128]{2,1,0:T(8,128)(2,1)S(1)}, u32[]{:S(2)}, u32[]{:S(2)}) async-start(bf16[8,32,128]{2,1,0:T(8,128)(2,1)} %bitcast.64), calls=%async_computation.5 | async-start | bytes 131072 | tf_op jit(solution)/shard_map/all_to_all | solution.py:167
  338.8 20.5 %all-to-all-start.1 = ((bf16[8,32,512]{2,1,0:T(8,128)(2,1)}), bf16[8,32,512]{2,1,0:T(8,128)(2,1)S(1)}, u32[]{:S(2)}, u32[]{:S(2)}) async-start(bf16[8,32,512]{2,1,0:T(8,128)(2,1)} %bitcast.44), calls=%async_computation.1 | async-start | bytes 524288 | tf_op jit(solution)/shard_map/all_to_all | solution.py:165
where the time goes:
time: 361 us; the launch traced here: 360 us
  waiting for transfers between devices  139 us (39%)
  starting transfers between devices  132 us (37%)
  local copies, waits for them, and re-layouts  76.9 us (21%)
  matrix products  6.8 us (2%)
  other arithmetic  4 us (1%)
    scatter x1, local copies, waits for them, and re-layouts, per_device(): inverse = jnp.zeros((length,), jnp.int32).at[where_to.reshape(-1)].set(so...  60.3 us
    ppermute x8, waiting for transfers between devices, shifted(): return lax.ppermute(block, axis, route)  57.1 us
    ppermute x8, starting transfers between devices, shifted(): return lax.ppermute(block, axis, route)  40.5 us
    ppermute x6, starting transfers between devices, from_behind(): return lax.ppermute(shard, axis, pairs)  37 us
    all_to_all x1, waiting for transfers between devices, per_device(): lax.all_to_all(pack_slots(query_grad), 'ctx', split_axis=0, concat_axis=0...  36.7 us
    all_to_all x1, starting transfers between devices, per_device(): lax.all_to_all(pack_slots(key_row_gradient), 'ctx', split_axis=0, concat_...  21.6 us
    all_to_all x1, waiting for transfers between devices, per_device(): lax.all_to_all(pack_slots(value_row_gradient), 'ctx', split_axis=0, conca...  16.4 us
    all_to_all x1, starting transfers between devices, per_device(): lax.all_to_all(pack_slots(value_row_gradient), 'ctx', split_axis=0, conca...  15.5 us
  transfers between devices with their start and end apart: 20, of which 11 were waited for; matrix products, arithmetic and copies ran while one was open for 23% of the time, Pallas kernels for 0%

commit v1 on v0

v1 whole, which is shorter than its diff:
```python
import jax
import jax.numpy as jnp
from jax import lax
from jax.sharding import PartitionSpec as P

HEAD_SIZE = 128
DOC_BLOCKS = 3


def from_behind(shard, axis, by):
    count = lax.axis_size(axis)
    pairs = [(i, i + by) for i in range(count) if 0 <= i + by < count]
    return lax.ppermute(shard, axis, pairs)


def block_grads(
    query_vectors,
    output_gradient,
    log_normalizer,
    row_correction,
    begins,
    query_pos,
    key_heads,
    value_heads,
    key_start,
):
    length = query_vectors.shape[0]
    scaling = HEAD_SIZE ** (-0.5)
    scores = (
        jnp.einsum("qngd,knd->qngk", query_vectors, key_heads, preferred_element_type=jnp.float32)
        * scaling
    )
    key_pos = key_start + lax.iota(jnp.int32, length)
    visible = (key_pos[None, :] <= query_pos[:, None]) & (key_pos[None, :] >= begins[:, None])
    weights = jnp.exp(
        jnp.where(visible[:, None, None, :], scores - log_normalizer[..., None], -jnp.inf)
    )
    weights_low = weights.astype(jnp.bfloat16)
    grad_weights = jnp.einsum(
        "qngd,knd->qngk", output_gradient, value_heads, preferred_element_type=jnp.float32
    )
    grad_scores = (weights * (grad_weights - row_correction[..., None]) * scaling).astype(
        jnp.bfloat16
    )
    query_term = jnp.einsum(
        "qngk,knd->qngd", grad_scores, key_heads, preferred_element_type=jnp.float32
    )
    key_term = jnp.einsum(
        "qngk,qngd->knd", grad_scores, query_vectors, preferred_element_type=jnp.float32
    )
    value_term = jnp.einsum(
        "qngk,qngd->knd", weights_low, output_gradient, preferred_element_type=jnp.float32
    )
    return query_term, key_term.reshape(length, -1), value_term.reshape(length, -1)


def per_device(
    query_head_rows,
    key_head_rows,
    value_head_rows,
    forward_output,
    cotangent,
    logsumexp,
    document_lengths,
    linear_row_index,
):
    length = query_head_rows.shape[0]
    kv_heads = key_head_rows.shape[1] // HEAD_SIZE
    kv_width = key_head_rows.shape[1]
    q_width = query_head_rows.shape[1]
    query_groups = logsumexp.shape[0] // kv_heads
    block_index = lax.axis_index("ctx")
    blocks = lax.axis_size("ctx")
    heads_axis = lax.axis_size("head")

    kv_own = jnp.concatenate([key_head_rows, value_head_rows], axis=1)
    kv_behind = [from_behind(kv_own, "ctx", d) for d in range(1, DOC_BLOCKS + 1)]

    query_pos = block_index * length + lax.iota(jnp.int32, length)
    finish = jnp.cumsum(document_lengths)
    firsts = finish - document_lengths
    begins = jnp.max(jnp.where(firsts[None, :] <= query_pos[:, None], firsts[None, :], 0), axis=1)
    query_vectors = query_head_rows.reshape(length, kv_heads, query_groups, HEAD_SIZE)
    output_gradient = cotangent.reshape(length, kv_heads, query_groups, HEAD_SIZE)
    log_normalizer = logsumexp.T.reshape(length, kv_heads, query_groups)
    row_correction = jnp.sum(
        output_gradient.astype(jnp.float32)
        * forward_output.reshape(length, kv_heads, query_groups, HEAD_SIZE).astype(jnp.float32),
        axis=3,
    )

    def block_terms(kv_part, distance):
        key_start = (block_index - distance) * length
        key_heads = kv_part[:, :kv_width].reshape(length, kv_heads, HEAD_SIZE)
        value_heads = kv_part[:, kv_width:].reshape(length, kv_heads, HEAD_SIZE)
        return block_grads(
            query_vectors,
            output_gradient,
            log_normalizer,
            row_correction,
            begins,
            query_pos,
            key_heads,
            value_heads,
            key_start,
        )

    query_acc, key_sum, value_sum = block_terms(kv_own, 0)
    returned = []
    for distance in range(1, DOC_BLOCKS + 1):
        query_term, key_term, value_term = block_terms(kv_behind[distance - 1], distance)
        query_acc = query_acc + query_term
        partial = jnp.concatenate([key_term, value_term], axis=1)
        returned.append(from_behind(partial, "ctx", -distance))
    for part in returned:
        key_sum = key_sum + part[:, :kv_width]
        value_sum = value_sum + part[:, kv_width:]

    rows = jnp.concatenate(
        [
            query_acc.reshape(length, -1).astype(jnp.bfloat16),
            key_sum.astype(jnp.bfloat16),
            value_sum.astype(jnp.bfloat16),
        ],
        axis=1,
    )
    width = rows.shape[1]

    capacity = 2 * length // blocks
    own_targets = lax.dynamic_slice_in_dim(linear_row_index, block_index * length, length)
    target = own_targets // length
    owner_marks = (target[:, None] == lax.iota(jnp.int32, blocks)[None, :]).astype(jnp.int32)
    slot_rank = jnp.sum(owner_marks * (jnp.cumsum(owner_marks, axis=0) - 1), axis=1)
    send_slots = target * capacity + slot_rank
    pack = (
        lax.iota(jnp.int32, blocks * capacity)[:, None] == send_slots[None, :]
    ).astype(jnp.bfloat16)
    packed = jnp.dot(pack, rows, preferred_element_type=jnp.float32).astype(jnp.bfloat16)

    arrived = lax.all_to_all(packed, "ctx", split_axis=0, concat_axis=0, tiled=True)

    all_owners = linear_row_index.reshape(blocks, length)
    landing = all_owners // length == block_index
    landed_rank = jnp.cumsum(landing.astype(jnp.int32), axis=1) - 1
    where_to = all_owners % length
    chosen = landing[:, :, None] & (
        landed_rank[:, :, None] == lax.iota(jnp.int32, capacity)[None, None, :]
    )
    slot_pos = jnp.sum(jnp.where(chosen, where_to[:, :, None], 0), axis=1).reshape(-1)
    slot_valid = jnp.any(chosen, axis=1).reshape(-1)
    unpack = (
        (lax.iota(jnp.int32, length)[:, None] == slot_pos[None, :]) & slot_valid[None, :]
    ).astype(jnp.bfloat16)
    linear_rows = jnp.dot(unpack, arrived, preferred_element_type=jnp.float32).astype(
        jnp.bfloat16
    )

    gathered = lax.all_to_all(linear_rows, "head", split_axis=0, concat_axis=1, tiled=True)
    sub = length // heads_axis
    gathered = gathered.reshape(sub, heads_axis, width)
    query_out = gathered[:, :, :q_width].reshape(sub, heads_axis * q_width)
    key_out = gathered[:, :, q_width : q_width + kv_width].reshape(sub, heads_axis * kv_width)
    value_out = gathered[:, :, q_width + kv_width :].reshape(sub, heads_axis * kv_width)
    return query_out, key_out, value_out


def solution(mesh):
    placed = (
        P("ctx", "head"),
        P("ctx", "head"),
        P("ctx", "head"),
        P("ctx", "head"),
        P("ctx", "head"),
        P("head", "ctx"),
        P(),
        P(),
    )
    return jax.shard_map(
        per_device,
        mesh=mesh,
        in_specs=placed,
        out_specs=(P(("ctx", "head"), None), P(("ctx", "head"), None), P(("ctx", "head"), None)),
        check_vma=False,
    )
```

time: 361 us -> 182 us (0.50)
  the two profiles are of different devices: /device:TPU:32 before, /device:TPU:2 now
where the time goes in v1:
time: 182 us
  starting transfers between devices  68.1 us (37%)
  waiting for transfers between devices  47.2 us (26%)
  blocking collectives  42.9 us (24%)
  other arithmetic  8 us (4%)
  matrix products  7.76 us (4%)
  local copies, waits for them, and re-layouts  6.65 us (4%)
    ppermute x6, starting transfers between devices, from_behind(): return lax.ppermute(shard, axis, pairs)  49 us
    all_to_all x1, blocking collectives, per_device(): lax.all_to_all(linear_rows, 'head', split_axis=0, concat_axis=1, tiled=True)  42.9 us
    ppermute x6, waiting for transfers between devices, from_behind(): return lax.ppermute(shard, axis, pairs)  24.7 us
    all_to_all x1, waiting for transfers between devices, per_device(): lax.all_to_all(packed, 'ctx', split_axis=0, concat_axis=0, tiled=True)  22.5 us
    all_to_all x1, starting transfers between devices, per_device(): lax.all_to_all(packed, 'ctx', split_axis=0, concat_axis=0, tiled=True)  19.1 us
  transfers between devices with their start and end apart: 7, of which 2 were waited for; matrix products, arithmetic and copies ran while one was open for 9% of the time, Pallas kernels for 0%

profile of v1, /device:TPU:2, one launch (start us, length us, event | category | flops | bytes accessed | tf_op | source)
XLA Modules:
  0.0 181.7 jit_solution(16785694982495848031)
XLA Ops:
  0.7 0.9 constant_dynamic-update-slice_fusion.1
  1.6 0.9 constant_dynamic-update-slice_fusion
  2.4 15.2 %collective-permute-start.2 = (bf16[256,256]{1,0:T(8,128)(2,1)S(1)}, bf16[256,256]{1,0:T(8,128)(2,1)S(1)}, u32[]{:S(2)}, u32[]{:S(2)}) collective-permute-start(bf16[256,256]{1,0:T(8,128)(2,1)S(1)} %constant_dynamic-update-slice_fusion), channel_id=1, source_target_pairs={{0,24},{8,32},{16,40},{24,48},{32,56},{40,64},{48,72},{56,80},{64,... | collective-permute-start | bytes 393224 | tf_op jit(solution)/shard_map/ppermute | solution.py:13
  17.6 2.5 %collective-permute-start.1 = (bf16[256,256]{1,0:T(8,128)(2,1)S(1)}, bf16[256,256]{1,0:T(8,128)(2,1)S(1)}, u32[]{:S(2)}, u32[]{:S(2)}) collective-permute-start(bf16[256,256]{1,0:T(8,128)(2,1)S(1)} %constant_dynamic-update-slice_fusion), channel_id=1, source_target_pairs={{0,16},{8,24},{16,32},{24,40},{32,48},{40,56},{48,64},{56,72},{64,... | collective-permute-start | bytes 393224 | tf_op jit(solution)/shard_map/ppermute | solution.py:13
  20.1 3.3 %collective-permute-start = (bf16[256,256]{1,0:T(8,128)(2,1)S(1)}, bf16[256,256]{1,0:T(8,128)(2,1)S(1)}, u32[]{:S(2)}, u32[]{:S(2)}) collective-permute-start(bf16[256,256]{1,0:T(8,128)(2,1)S(1)} %constant_dynamic-update-slice_fusion), channel_id=1, source_target_pairs={{0,8},{8,16},{16,24},{24,32},{32,40},{40,48},{48,56},{56,64},{64,7... | collective-permute-start | bytes 393224 | tf_op jit(solution)/shard_map/ppermute | solution.py:13
  23.4 0.8 fusion.111
  24.2 0.8 and_select_fusion
  24.9 0.7 copy.130
  25.7 0.1 reduce-window.33
  25.8 0.1 reduce.4
  25.9 0.7 sub.124
  26.6 0.6 reduce-window.31
  27.2 0.2 slice_reduce_fusion
  27.4 0.1 fusion.75
  27.5 0.8 multiply_add_fusion
  28.3 1.1 copy.187
  29.4 0.1 copy.188
  29.6 0.1 convert_multiply_fusion
  29.7 0.2 mul.93
  29.8 0.3 reduce_sum.29
  30.2 0.0 copy-start.4
  30.2 0.1 copy.133
  30.3 0.1 select_reduce_fusion.1
  30.4 0.3 compare_and_fusion.2
  30.7 0.4 fusion.23
  31.1 0.3 fusion.41
  31.4 0.3 convolution_bitcast_fusion.4
  31.6 0.3 convolution_bitcast_fusion.5
  32.0 0.4 fusion.35
  32.3 0.3 convolution_bitcast_fusion.6
  32.7 0.3 fusion.44
  32.9 0.3 convolution_bitcast_fusion.7
  33.3 14.0 %collective-permute-start.5 = (f32[256,256]{0,1:T(8,128)S(1)}, f32[256,256]{0,1:T(8,128)S(1)}, u32[]{:S(2)}, u32[]{:S(2)}) collective-permute-start(f32[256,256]{0,1:T(8,128)S(1)} %pad_maximum_fusion.2), channel_id=1, source_target_pairs={{24,0},{32,8},{40,16},{48,24},{56,32},{64,40},{72,48},{80,56},{88,... | collective-permute-start | bytes 786440 | tf_op jit(solution)/shard_map/ppermute | solution.py:13
  47.3 0.4 fusion.31
  47.6 0.3 convolution_bitcast_fusion.8
  48.0 0.3 fusion.43
  48.3 0.3 convolution_bitcast_fusion.9
  48.6 2.8 %collective-permute-start.4 = (f32[256,256]{0,1:T(8,128)S(1)}, f32[256,256]{0,1:T(8,128)S(1)}, u32[]{:S(2)}, u32[]{:S(2)}) collective-permute-start(f32[256,256]{0,1:T(8,128)S(1)} %pad_maximum_fusion.1), channel_id=1, source_target_pairs={{16,0},{24,8},{32,16},{40,24},{48,32},{56,40},{64,48},{72,56},{80,... | collective-permute-start | bytes 786440 | tf_op jit(solution)/shard_map/ppermute | solution.py:13
  51.4 0.4 fusion.27
  51.8 0.3 convolution_bitcast_fusion.10
  52.1 0.3 fusion.42
  52.4 0.3 convolution_bitcast_fusion.11
  52.7 11.2 %collective-permute-start.3 = (f32[256,256]{0,1:T(8,128)S(1)}, f32[256,256]{0,1:T(8,128)S(1)}, u32[]{:S(2)}, u32[]{:S(2)}) collective-permute-start(f32[256,256]{0,1:T(8,128)S(1)} %pad_maximum_fusion), channel_id=1, source_target_pairs={{8,0},{16,8},{24,16},{32,24},{40,32},{48,40},{56,48},{64,56},{72,6... | collective-permute-start | bytes 786440 | tf_op jit(solution)/shard_map/ppermute | solution.py:13
  64.0 0.2 fusion.84
  64.2 0.3 fusion.83
  64.5 0.3 fusion.47
  64.8 24.7 %collective-permute-done.4 = f32[256,256]{0,1:T(8,128)S(1)} collective-permute-done((f32[256,256]{0,1:T(8,128)S(1)}, f32[256,256]{0,1:T(8,128)S(1)}, u32[]{:S(2)}, u32[]{:S(2)}) %collective-permute-start.4) | collective-permute-done | bytes 262176 | tf_op jit(solution)/shard_map/ppermute | solution.py:13
  89.5 0.3 fusion.70
  89.8 1.3 fusion.40
  91.1 19.1 %all-to-all-start = ((bf16[64,8,768]{2,1,0:T(8,128)(2,1)}), bf16[64,8,768]{2,1,0:T(8,128)(2,1)S(1)}, u32[]{:S(2)}, u32[]{:S(2)}) async-start(bf16[64,8,768]{2,1,0:T(8,128)(2,1)} %fusion.40), calls=%async_computation | async-start | bytes 1572864 | tf_op jit(solution)/shard_map/all_to_all | solution.py:140
  110.3 0.6 reduce-window.24
  110.9 0.2 slice_reduce_fusion.1
  111.2 0.1 fusion.71
  111.3 0.1 copy_bitcast_fusion.2
  111.3 1.2 select_reduce_fusion
  112.5 0.1 eq.89
  112.6 1.2 fusion.60
  113.8 0.1 and.86
  113.9 22.5 %all-to-all-done = bf16[64,8,768]{2,1,0:T(8,128)(2,1)S(1)} async-done(((bf16[64,8,768]{2,1,0:T(8,128)(2,1)}), bf16[64,8,768]{2,1,0:T(8,128)(2,1)S(1)}, u32[]{:S(2)}, u32[]{:S(2)}) %all-to-all-start) | async-done | bytes 786464 | tf_op jit(solution)/shard_map/all_to_all | solution.py:140
  136.4 0.4 convolution_convert_fusion.1
  136.8 42.9 %all_to_all.28 = bf16[8,32,768]{2,1,0:T(8,128)(2,1)S(1)} all-to-all(bf16[8,32,768]{2,1,0:T(8,128)(2,1)S(1)} %bitcast.325), channel_id=1, replica_groups=mesh['ctx'=64,'head'=8] {'head'}, dimensions={0} | all-to-all | bytes 786432 | tf_op jit(solution)/shard_map/all_to_all | solution.py:158
  179.7 0.7 copy.191
  180.4 0.6 copy.199
  181.1 0.6 copy.200
  (31 shorter events, 0.3 us)
Async XLA Ops:
  0.6 28.8 %copy-start = (bf16[256,512]{1,0:T(8,128)(2,1)S(1)}, bf16[256,512]{1,0:T(8,128)(2,1)}, u32[]{:S(2)}) copy-start(bf16[256,512]{1,0:T(8,128)(2,1)} %param.12) | copy-start | bytes 786436
  0.6 28.9 %copy-start.3 = (bf16[256,512]{1,0:T(8,128)(2,1)S(1)}, bf16[256,512]{1,0:T(8,128)(2,1)}, u32[]{:S(2)}) copy-start(bf16[256,512]{1,0:T(8,128)(2,1)} %param.11) | copy-start | bytes 786436
  2.4 29.5 %collective-permute-start.2 = (bf16[256,256]{1,0:T(8,128)(2,1)S(1)}, bf16[256,256]{1,0:T(8,128)(2,1)S(1)}, u32[]{:S(2)}, u32[]{:S(2)}) collective-permute-start(bf16[256,256]{1,0:T(8,128)(2,1)S(1)} %constant_dynamic-update-slice_fusion), channel_id=1, source_target_pairs={{0,24},{8,32},{16,40},{24,48},{32,56},{40,64},{48,72},{56,80},{64,... | collective-permute-start | bytes 393224 | tf_op jit(solution)/shard_map/ppermute | solution.py:13
  17.6 29.7 %collective-permute-start.1 = (bf16[256,256]{1,0:T(8,128)(2,1)S(1)}, bf16[256,256]{1,0:T(8,128)(2,1)S(1)}, u32[]{:S(2)}, u32[]{:S(2)}) collective-permute-start(bf16[256,256]{1,0:T(8,128)(2,1)S(1)} %constant_dynamic-update-slice_fusion), channel_id=1, source_target_pairs={{0,16},{8,24},{16,32},{24,40},{32,48},{40,56},{48,64},{56,72},{64,... | collective-permute-start | bytes 393224 | tf_op jit(solution)/shard_map/ppermute | solution.py:13
  20.1 31.3 %collective-permute-start = (bf16[256,256]{1,0:T(8,128)(2,1)S(1)}, bf16[256,256]{1,0:T(8,128)(2,1)S(1)}, u32[]{:S(2)}, u32[]{:S(2)}) collective-permute-start(bf16[256,256]{1,0:T(8,128)(2,1)S(1)} %constant_dynamic-update-slice_fusion), channel_id=1, source_target_pairs={{0,8},{8,16},{16,24},{24,32},{32,40},{40,48},{48,56},{56,64},{64,7... | collective-permute-start | bytes 393224 | tf_op jit(solution)/shard_map/ppermute | solution.py:13
  29.6 1.0 copy-start.2
  29.6 1.0 copy-start.5
  30.2 0.9 copy-start.4
  33.3 31.5 %collective-permute-start.5 = (f32[256,256]{0,1:T(8,128)S(1)}, f32[256,256]{0,1:T(8,128)S(1)}, u32[]{:S(2)}, u32[]{:S(2)}) collective-permute-start(f32[256,256]{0,1:T(8,128)S(1)} %pad_maximum_fusion.2), channel_id=1, source_target_pairs={{24,0},{32,8},{40,16},{48,24},{56,32},{64,40},{72,48},{80,56},{88,... | collective-permute-start | bytes 786440 | tf_op jit(solution)/shard_map/ppermute | solution.py:13
  48.6 40.9 %collective-permute-start.4 = (f32[256,256]{0,1:T(8,128)S(1)}, f32[256,256]{0,1:T(8,128)S(1)}, u32[]{:S(2)}, u32[]{:S(2)}) collective-permute-start(f32[256,256]{0,1:T(8,128)S(1)} %pad_maximum_fusion.1), channel_id=1, source_target_pairs={{16,0},{24,8},{32,16},{40,24},{48,32},{56,40},{64,48},{72,56},{80,... | collective-permute-start | bytes 786440 | tf_op jit(solution)/shard_map/ppermute | solution.py:13
  52.7 36.7 %collective-permute-start.3 = (f32[256,256]{0,1:T(8,128)S(1)}, f32[256,256]{0,1:T(8,128)S(1)}, u32[]{:S(2)}, u32[]{:S(2)}) collective-permute-start(f32[256,256]{0,1:T(8,128)S(1)} %pad_maximum_fusion), channel_id=1, source_target_pairs={{8,0},{16,8},{24,16},{32,24},{40,32},{48,40},{56,48},{64,56},{72,6... | collective-permute-start | bytes 786440 | tf_op jit(solution)/shard_map/ppermute | solution.py:13
  91.1 19.1 %copy-start.1 = (s32[16384]{0:T(1024)S(1)}, s32[16384]{0:T(1024)}, u32[]{:S(2)}) copy-start(s32[16384]{0:T(1024)} %param.15) | copy-start | bytes 196612
  91.1 45.3 %all-to-all-start = ((bf16[64,8,768]{2,1,0:T(8,128)(2,1)}), bf16[64,8,768]{2,1,0:T(8,128)(2,1)S(1)}, u32[]{:S(2)}, u32[]{:S(2)}) async-start(bf16[64,8,768]{2,1,0:T(8,128)(2,1)} %fusion.40), calls=%async_computation | async-start | bytes 1572864 | tf_op jit(solution)/shard_map/all_to_all | solution.py:140

commit v2 on v1

--- a/solution.py
+++ b/solution.py
@@ -110,11 +110,11 @@
     for distance in range(1, DOC_BLOCKS + 1):
         query_term, key_term, value_term = block_terms(kv_behind[distance - 1], distance)
         query_acc = query_acc + query_term
-        partial = jnp.concatenate([key_term, value_term], axis=1)
+        partial = jnp.concatenate([key_term, value_term], axis=1).astype(jnp.bfloat16)
         returned.append(from_behind(partial, "ctx", -distance))
     for part in returned:
-        key_sum = key_sum + part[:, :kv_width]
-        value_sum = value_sum + part[:, kv_width:]
+        key_sum = key_sum + part[:, :kv_width].astype(jnp.float32)
+        value_sum = value_sum + part[:, kv_width:].astype(jnp.float32)
 
     rows = jnp.concatenate(
         [

time: 182 us -> 169 us (0.929)
  blocking collectives: 42.9 us -> 32.7 us
  waiting for transfers between devices: 47.2 us -> 45.2 us
    ppermute x6, waiting for transfers between devices: 24.7 us -> 8.84 us  [from_behind(): return lax.ppermute(shard, axis, pairs)]
    all_to_all x1, waiting for transfers between devices: 22.5 us -> 36.3 us  [per_device(): lax.all_to_all(packed, 'ctx', split_axis=0, concat_axis=0, tiled=True)]
    all_to_all x1, blocking collectives: 42.9 us -> 32.7 us  [per_device(): lax.all_to_all(linear_rows, 'head', split_axis=0, concat_axis=1, tiled=True)]
  transfers between devices with their start and end apart: 7 -> 7, of which waited for: 2 -> 2; matrix products, arithmetic and copies ran while one was open for 9% -> 10% of each run, Pallas kernels for 0% -> 0%
where the time goes in v2:
time: 169 us
  starting transfers between devices  67.3 us (40%)
  waiting for transfers between devices  45.2 us (27%)
  blocking collectives  32.7 us (19%)
  other arithmetic  7.97 us (5%)
  matrix products  7.75 us (5%)
  local copies, waits for them, and re-layouts  6.65 us (4%)
    ppermute x6, starting transfers between devices, from_behind(): return lax.ppermute(shard, axis, pairs)  49 us
    all_to_all x1, waiting for transfers between devices, per_device(): lax.all_to_all(packed, 'ctx', split_axis=0, concat_axis=0, tiled=True)  36.3 us
    all_to_all x1, blocking collectives, per_device(): lax.all_to_all(linear_rows, 'head', split_axis=0, concat_axis=1, tiled=True)  32.7 us
    all_to_all x1, starting transfers between devices, per_device(): lax.all_to_all(packed, 'ctx', split_axis=0, concat_axis=0, tiled=True)  18.3 us
    ppermute x6, waiting for transfers between devices, from_behind(): return lax.ppermute(shard, axis, pairs)  8.84 us
  transfers between devices with their start and end apart: 7, of which 2 were waited for; matrix products, arithmetic and copies ran while one was open for 10% of the time, Pallas kernels for 0%

profile of v2, /device:TPU:2, one launch (start us, length us, event | category | flops | bytes accessed | tf_op | source)
XLA Modules:
  0.0 168.7 jit_solution(5422373578759134068)
XLA Ops:
  0.7 0.9 constant_dynamic-update-slice_fusion.1
  1.6 0.9 constant_dynamic-update-slice_fusion
  2.4 15.2 %collective-permute-start.2 = (bf16[256,256]{1,0:T(8,128)(2,1)S(1)}, bf16[256,256]{1,0:T(8,128)(2,1)S(1)}, u32[]{:S(2)}, u32[]{:S(2)}) collective-permute-start(bf16[256,256]{1,0:T(8,128)(2,1)S(1)} %constant_dynamic-update-slice_fusion), channel_id=1, source_target_pairs={{0,24},{8,32},{16,40},{24,48},{32,56},{40,64},{48,72},{56,80},{64,... | collective-permute-start | bytes 393224 | tf_op jit(solution)/shard_map/ppermute | solution.py:13
  17.6 2.5 %collective-permute-start.1 = (bf16[256,256]{1,0:T(8,128)(2,1)S(1)}, bf16[256,256]{1,0:T(8,128)(2,1)S(1)}, u32[]{:S(2)}, u32[]{:S(2)}) collective-permute-start(bf16[256,256]{1,0:T(8,128)(2,1)S(1)} %constant_dynamic-update-slice_fusion), channel_id=1, source_target_pairs={{0,16},{8,24},{16,32},{24,40},{32,48},{40,56},{48,64},{56,72},{64,... | collective-permute-start | bytes 393224 | tf_op jit(solution)/shard_map/ppermute | solution.py:13
  20.1 3.3 %collective-permute-start = (bf16[256,256]{1,0:T(8,128)(2,1)S(1)}, bf16[256,256]{1,0:T(8,128)(2,1)S(1)}, u32[]{:S(2)}, u32[]{:S(2)}) collective-permute-start(bf16[256,256]{1,0:T(8,128)(2,1)S(1)} %constant_dynamic-update-slice_fusion), channel_id=1, source_target_pairs={{0,8},{8,16},{16,24},{24,32},{32,40},{40,48},{48,56},{56,64},{64,7... | collective-permute-start | bytes 393224 | tf_op jit(solution)/shard_map/ppermute | solution.py:13
  23.4 0.8 fusion.115
  24.2 0.8 and_select_fusion
  24.9 0.7 copy.130
  25.7 0.1 reduce-window.33
  25.8 0.1 reduce.4
  25.9 0.7 sub.124
  26.6 0.6 reduce-window.31
  27.2 0.2 slice_reduce_fusion
  27.4 0.1 fusion.79
  27.5 0.8 multiply_add_fusion
  28.3 1.1 copy.187
  29.4 0.1 copy.188
  29.6 0.1 convert_multiply_fusion
  29.7 0.2 mul.93
  29.8 0.3 reduce_sum.29
  30.2 0.0 copy-start.4
  30.2 0.1 copy.133
  30.3 0.1 select_reduce_fusion.1
  30.4 0.3 compare_and_fusion.2
  30.7 0.4 fusion.23
  31.1 0.3 fusion.41
  31.4 0.3 convolution_bitcast_fusion.4
  31.6 0.3 convolution_bitcast_fusion.5
  32.0 0.4 fusion.35
  32.3 0.3 fusion.53
  32.7 0.3 fusion.44
  32.9 0.3 fusion.52
  33.3 14.0 %collective-permute-start.5 = (bf16[256,256]{0,1:T(8,128)(2,1)S(1)}, bf16[256,256]{0,1:T(8,128)(2,1)S(1)}, u32[]{:S(2)}, u32[]{:S(2)}) collective-permute-start(bf16[256,256]{0,1:T(8,128)(2,1)S(1)} %pad_maximum_fusion.2), channel_id=1, source_target_pairs={{24,0},{32,8},{40,16},{48,24},{56,32},{64,40},{72,48},{80,56},{88,... | collective-permute-start | bytes 393224 | tf_op jit(solution)/shard_map/ppermute | solution.py:13
  47.3 0.4 fusion.31
  47.6 0.3 fusion.51
  48.0 0.3 fusion.43
  48.2 0.3 fusion.50
  48.6 2.8 %collective-permute-start.4 = (bf16[256,256]{0,1:T(8,128)(2,1)S(1)}, bf16[256,256]{0,1:T(8,128)(2,1)S(1)}, u32[]{:S(2)}, u32[]{:S(2)}) collective-permute-start(bf16[256,256]{0,1:T(8,128)(2,1)S(1)} %pad_maximum_fusion.1), channel_id=1, source_target_pairs={{16,0},{24,8},{32,16},{40,24},{48,32},{56,40},{64,48},{72,56},{80,... | collective-permute-start | bytes 393224 | tf_op jit(solution)/shard_map/ppermute | solution.py:13
  51.4 0.4 fusion.27
  51.8 0.3 fusion.49
  52.1 0.3 fusion.42
  52.4 0.3 fusion.48
  52.7 11.2 %collective-permute-start.3 = (bf16[256,256]{0,1:T(8,128)(2,1)S(1)}, bf16[256,256]{0,1:T(8,128)(2,1)S(1)}, u32[]{:S(2)}, u32[]{:S(2)}) collective-permute-start(bf16[256,256]{0,1:T(8,128)(2,1)S(1)} %pad_maximum_fusion), channel_id=1, source_target_pairs={{8,0},{16,8},{24,16},{32,24},{40,32},{48,40},{56,48},{64,56},{72,6... | collective-permute-start | bytes 393224 | tf_op jit(solution)/shard_map/ppermute | solution.py:13
  63.9 0.2 fusion.88
  64.2 0.3 fusion.87
  64.5 0.3 fusion.47
  64.7 8.8 %collective-permute-done.3 = bf16[256,256]{0,1:T(8,128)(2,1)S(1)} collective-permute-done((bf16[256,256]{0,1:T(8,128)(2,1)S(1)}, bf16[256,256]{0,1:T(8,128)(2,1)S(1)}, u32[]{:S(2)}, u32[]{:S(2)}) %collective-permute-start.3) | collective-permute-done | bytes 131104 | tf_op jit(solution)/shard_map/ppermute | solution.py:13
  73.6 0.3 add_convert_fusion.1
  73.9 1.3 fusion.40
  75.2 18.3 %all-to-all-start = ((bf16[64,8,768]{2,1,0:T(8,128)(2,1)}), bf16[64,8,768]{2,1,0:T(8,128)(2,1)S(1)}, u32[]{:S(2)}, u32[]{:S(2)}) async-start(bf16[64,8,768]{2,1,0:T(8,128)(2,1)} %fusion.40), calls=%async_computation | async-start | bytes 1572864 | tf_op jit(solution)/shard_map/all_to_all | solution.py:140
  93.6 0.6 reduce-window.24
  94.2 0.2 slice_reduce_fusion.1
  94.5 0.1 fusion.75
  94.6 0.1 copy_bitcast_fusion.2
  94.7 1.2 select_reduce_fusion
  95.8 0.1 eq.89
  95.9 1.2 fusion.66
  97.1 0.1 and.86
  97.2 36.3 %all-to-all-done = bf16[64,8,768]{2,1,0:T(8,128)(2,1)S(1)} async-done(((bf16[64,8,768]{2,1,0:T(8,128)(2,1)}), bf16[64,8,768]{2,1,0:T(8,128)(2,1)S(1)}, u32[]{:S(2)}, u32[]{:S(2)}) %all-to-all-start) | async-done | bytes 786464 | tf_op jit(solution)/shard_map/all_to_all | solution.py:140
  133.5 0.4 convolution_convert_fusion.1
  133.9 32.7 %all_to_all.28 = bf16[8,32,768]{2,1,0:T(8,128)(2,1)S(1)} all-to-all(bf16[8,32,768]{2,1,0:T(8,128)(2,1)S(1)} %bitcast.337), channel_id=1, replica_groups=mesh['ctx'=64,'head'=8] {'head'}, dimensions={0} | all-to-all | bytes 786432 | tf_op jit(solution)/shard_map/all_to_all | solution.py:158
  166.7 0.7 copy.191
  167.4 0.6 copy.199
  168.0 0.6 copy.200
  (31 shorter events, 0.3 us)
Async XLA Ops:
  0.6 28.8 %copy-start = (bf16[256,512]{1,0:T(8,128)(2,1)S(1)}, bf16[256,512]{1,0:T(8,128)(2,1)}, u32[]{:S(2)}) copy-start(bf16[256,512]{1,0:T(8,128)(2,1)} %param.12) | copy-start | bytes 786436
  0.6 28.9 %copy-start.3 = (bf16[256,512]{1,0:T(8,128)(2,1)S(1)}, bf16[256,512]{1,0:T(8,128)(2,1)}, u32[]{:S(2)}) copy-start(bf16[256,512]{1,0:T(8,128)(2,1)} %param.11) | copy-start | bytes 786436
  2.4 29.5 %collective-permute-start.2 = (bf16[256,256]{1,0:T(8,128)(2,1)S(1)}, bf16[256,256]{1,0:T(8,128)(2,1)S(1)}, u32[]{:S(2)}, u32[]{:S(2)}) collective-permute-start(bf16[256,256]{1,0:T(8,128)(2,1)S(1)} %constant_dynamic-update-slice_fusion), channel_id=1, source_target_pairs={{0,24},{8,32},{16,40},{24,48},{32,56},{40,64},{48,72},{56,80},{64,... | collective-permute-start | bytes 393224 | tf_op jit(solution)/shard_map/ppermute | solution.py:13
  17.6 29.7 %collective-permute-start.1 = (bf16[256,256]{1,0:T(8,128)(2,1)S(1)}, bf16[256,256]{1,0:T(8,128)(2,1)S(1)}, u32[]{:S(2)}, u32[]{:S(2)}) collective-permute-start(bf16[256,256]{1,0:T(8,128)(2,1)S(1)} %constant_dynamic-update-slice_fusion), channel_id=1, source_target_pairs={{0,16},{8,24},{16,32},{24,40},{32,48},{40,56},{48,64},{56,72},{64,... | collective-permute-start | bytes 393224 | tf_op jit(solution)/shard_map/ppermute | solution.py:13
  20.1 31.3 %collective-permute-start = (bf16[256,256]{1,0:T(8,128)(2,1)S(1)}, bf16[256,256]{1,0:T(8,128)(2,1)S(1)}, u32[]{:S(2)}, u32[]{:S(2)}) collective-permute-start(bf16[256,256]{1,0:T(8,128)(2,1)S(1)} %constant_dynamic-update-slice_fusion), channel_id=1, source_target_pairs={{0,8},{8,16},{16,24},{24,32},{32,40},{40,48},{48,56},{56,64},{64,7... | collective-permute-start | bytes 393224 | tf_op jit(solution)/shard_map/ppermute | solution.py:13
  29.6 1.0 copy-start.2
  29.6 1.0 copy-start.5
  30.2 0.9 copy-start.4
  33.3 31.4 %collective-permute-start.5 = (bf16[256,256]{0,1:T(8,128)(2,1)S(1)}, bf16[256,256]{0,1:T(8,128)(2,1)S(1)}, u32[]{:S(2)}, u32[]{:S(2)}) collective-permute-start(bf16[256,256]{0,1:T(8,128)(2,1)S(1)} %pad_maximum_fusion.2), channel_id=1, source_target_pairs={{24,0},{32,8},{40,16},{48,24},{56,32},{64,40},{72,48},{80,56},{88,... | collective-permute-start | bytes 393224 | tf_op jit(solution)/shard_map/ppermute | solution.py:13
  48.6 16.2 %collective-permute-start.4 = (bf16[256,256]{0,1:T(8,128)(2,1)S(1)}, bf16[256,256]{0,1:T(8,128)(2,1)S(1)}, u32[]{:S(2)}, u32[]{:S(2)}) collective-permute-start(bf16[256,256]{0,1:T(8,128)(2,1)S(1)} %pad_maximum_fusion.1), channel_id=1, source_target_pairs={{16,0},{24,8},{32,16},{40,24},{48,32},{56,40},{64,48},{72,56},{80,... | collective-permute-start | bytes 393224 | tf_op jit(solution)/shard_map/ppermute | solution.py:13
  52.7 20.9 %collective-permute-start.3 = (bf16[256,256]{0,1:T(8,128)(2,1)S(1)}, bf16[256,256]{0,1:T(8,128)(2,1)S(1)}, u32[]{:S(2)}, u32[]{:S(2)}) collective-permute-start(bf16[256,256]{0,1:T(8,128)(2,1)S(1)} %pad_maximum_fusion), channel_id=1, source_target_pairs={{8,0},{16,8},{24,16},{32,24},{40,32},{48,40},{56,48},{64,56},{72,6... | collective-permute-start | bytes 393224 | tf_op jit(solution)/shard_map/ppermute | solution.py:13
  75.2 18.4 %copy-start.1 = (s32[16384]{0:T(1024)S(1)}, s32[16384]{0:T(1024)}, u32[]{:S(2)}) copy-start(s32[16384]{0:T(1024)} %param.15) | copy-start | bytes 196612
  75.2 58.3 %all-to-all-start = ((bf16[64,8,768]{2,1,0:T(8,128)(2,1)}), bf16[64,8,768]{2,1,0:T(8,128)(2,1)S(1)}, u32[]{:S(2)}, u32[]{:S(2)}) async-start(bf16[64,8,768]{2,1,0:T(8,128)(2,1)} %fusion.40), calls=%async_computation | async-start | bytes 1572864 | tf_op jit(solution)/shard_map/all_to_all | solution.py:140

commit v3 on v2

--- a/solution.py
+++ b/solution.py
@@ -74,7 +74,19 @@
     heads_axis = lax.axis_size("head")
 
     kv_own = jnp.concatenate([key_head_rows, value_head_rows], axis=1)
-    kv_behind = [from_behind(kv_own, "ctx", d) for d in range(1, DOC_BLOCKS + 1)]
+    even = block_index % 2 == 0
+    partner = [(i, i ^ 1) for i in range(blocks)]
+    kv_two = from_behind(kv_own, "ctx", 2)
+    kv_partner_own = lax.ppermute(kv_own, "ctx", [(i, i + 1) for i in range(0, blocks, 2)])
+    kv_partner_two = lax.ppermute(kv_two, "ctx", partner)
+    kv_three = lax.ppermute(
+        kv_own, "ctx", [(i, i + 3) for i in range(1, blocks, 2) if i + 3 < blocks]
+    )
+    kv_behind = [
+        jnp.where(even, kv_partner_two, kv_partner_own),
+        kv_two,
+        jnp.where(even, kv_three, kv_partner_two),
+    ]
 
     query_pos = block_index * length + lax.iota(jnp.int32, length)
     finish = jnp.cumsum(document_lengths)
@@ -106,15 +118,21 @@
         )
 
     query_acc, key_sum, value_sum = block_terms(kv_own, 0)
-    returned = []
+    partials = []
     for distance in range(1, DOC_BLOCKS + 1):
         query_term, key_term, value_term = block_terms(kv_behind[distance - 1], distance)
         query_acc = query_acc + query_term
-        partial = jnp.concatenate([key_term, value_term], axis=1).astype(jnp.bfloat16)
-        returned.append(from_behind(partial, "ctx", -distance))
-    for part in returned:
-        key_sum = key_sum + part[:, :kv_width].astype(jnp.float32)
-        value_sum = value_sum + part[:, kv_width:].astype(jnp.float32)
+        partials.append(jnp.concatenate([key_term, value_term], axis=1))
+    swapped = lax.ppermute(jnp.where(even, partials[0], partials[2]), "ctx", partner)
+    to_partner = lax.ppermute(partials[0], "ctx", [(i, i - 1) for i in range(1, blocks, 2)])
+    crossed = from_behind((partials[1] + swapped).astype(jnp.bfloat16), "ctx", -2)
+    from_three = lax.ppermute(
+        partials[2].astype(jnp.bfloat16), "ctx", [(i, i - 3) for i in range(0, blocks, 2) if i >= 3]
+    )
+    own_sum = jnp.concatenate([key_sum, value_sum], axis=1) + crossed.astype(jnp.float32)
+    own_sum = own_sum + jnp.where(even, to_partner, from_three.astype(jnp.float32))
+    key_sum = own_sum[:, :kv_width]
+    value_sum = own_sum[:, kv_width:]
 
     rows = jnp.concatenate(
         [

time: 169 us -> 166 us (0.982)
  waiting for transfers between devices: 45.2 us -> 37.9 us
  starting transfers between devices: 67.3 us -> 70.2 us
    ppermute x6 -> x2, starting transfers between devices: 49 us -> 29.4 us  [from_behind(): return lax.ppermute(shard, axis, pairs)]
    ppermute x0 -> x6, starting transfers between devices: none -> 14.9 us  [the longest x1 4.22 us: per_device(): lax.ppermute(partials[2].astype(jnp.bfloat16), 'ctx', [(i, i - 3) for i i...]
    all_to_all x1, starting transfers between devices: 18.3 us -> 25.9 us  [per_device(): lax.all_to_all(packed, 'ctx', split_axis=0, concat_axis=0, tiled=True)]
    ppermute x6 -> x2, waiting for transfers between devices: 8.84 us -> 3.72 us  [from_behind(): return lax.ppermute(shard, axis, pairs)]
    all_to_all x1, waiting for transfers between devices: 36.3 us -> 33.7 us  [per_device(): lax.all_to_all(packed, 'ctx', split_axis=0, concat_axis=0, tiled=True)]
  transfers between devices with their start and end apart: 7 -> 9, of which waited for: 2 -> 3; matrix products, arithmetic and copies ran while one was open for 10% -> 9% of each run, Pallas kernels for 0% -> 0%
where the time goes in v3:
time: 166 us; the launch traced here: 165 us
  starting transfers between devices  70.2 us (42%)
  waiting for transfers between devices  37.9 us (23%)
  blocking collectives  32.6 us (20%)
  other arithmetic  8.1 us (5%)
  matrix products  7.69 us (5%)
  local copies, waits for them, and re-layouts  7.27 us (4%)
    all_to_all x1, waiting for transfers between devices, per_device(): lax.all_to_all(packed, 'ctx', split_axis=0, concat_axis=0, tiled=True)  33.7 us
    all_to_all x1, blocking collectives, per_device(): lax.all_to_all(linear_rows, 'head', split_axis=0, concat_axis=1, tiled=True)  32.6 us
    ppermute x2, starting transfers between devices, from_behind(): return lax.ppermute(shard, axis, pairs)  29.4 us
    all_to_all x1, starting transfers between devices, per_device(): lax.all_to_all(packed, 'ctx', split_axis=0, concat_axis=0, tiled=True)  25.9 us
    ppermute x1, starting transfers between devices, per_device(): lax.ppermute(partials[2].astype(jnp.bfloat16), 'ctx', [(i, i - 3) for i i...  4.22 us
    ppermute x1, starting transfers between devices, per_device(): lax.ppermute(kv_own, 'ctx', [(i, i + 1) for i in range(0, blocks, 2)])  4.22 us
    ppermute x2, waiting for transfers between devices, from_behind(): return lax.ppermute(shard, axis, pairs)  3.72 us
  transfers between devices with their start and end apart: 9, of which 3 were waited for; matrix products, arithmetic and copies ran while one was open for 9% of the time, Pallas kernels for 0%

profile of v3, /device:TPU:2, one launch (start us, length us, event | category | flops | bytes accessed | tf_op | source)
XLA Modules:
  0.0 164.9 jit_solution(10158905778790915014)
XLA Ops:
  0.7 0.9 constant_dynamic-update-slice_fusion.1
  1.6 0.9 constant_dynamic-update-slice_fusion
  2.4 1.3 collective-permute-start.3
  3.7 4.2 %collective-permute-start.2 = (bf16[256,256]{1,0:T(8,128)(2,1)S(1)}, bf16[256,256]{1,0:T(8,128)(2,1)S(1)}, u32[]{:S(2)}, u32[]{:S(2)}) collective-permute-start(bf16[256,256]{1,0:T(8,128)(2,1)S(1)} %constant_dynamic-update-slice_fusion), channel_id=1, source_target_pairs={{0,8},{16,24},{32,40},{48,56},{64,72},{80,88},{96,104},{112,120},{... | collective-permute-start | bytes 393224 | tf_op jit(solution)/shard_map/ppermute | solution.py:80
  8.0 15.7 %collective-permute-start = (bf16[256,256]{1,0:T(8,128)(2,1)S(1)}, bf16[256,256]{1,0:T(8,128)(2,1)S(1)}, u32[]{:S(2)}, u32[]{:S(2)}) collective-permute-start(bf16[256,256]{1,0:T(8,128)(2,1)S(1)} %constant_dynamic-update-slice_fusion), channel_id=1, source_target_pairs={{0,16},{8,24},{16,32},{24,40},{32,48},{40,56},{48,64},{56,72},{64,... | collective-permute-start | bytes 393224 | tf_op jit(solution)/shard_map/ppermute | solution.py:13
  23.7 0.8 fusion.110
  24.5 0.8 and_select_fusion
  25.2 0.7 copy.141
  26.0 0.1 reduce-window.33
  26.1 0.1 reduce.4
  26.2 0.7 sub.124
  26.9 0.6 reduce-window.31
  27.5 0.2 slice_reduce_fusion
  27.7 0.1 fusion.75
  27.8 0.8 multiply_add_fusion
  28.6 1.1 copy.223
  29.7 0.1 copy.224
  29.9 0.2 mul.93
  30.1 0.3 reduce_sum.29
  30.6 0.1 select_reduce_fusion.1
  30.7 0.3 compare_and_fusion.1
  31.0 0.4 fusion.23
  31.3 0.3 convolution_bitcast_fusion.11
  31.7 0.5 copy-done.4
  32.2 0.3 fusion.41
  32.5 0.3 convolution_bitcast_fusion.4
  32.7 0.3 convolution_bitcast_fusion.12
  33.1 0.4 fusion.31
  33.4 0.3 convolution_bitcast_fusion.9
  33.7 1.9 %collective-permute-start.1 = (bf16[256,256]{1,0:T(8,128)(2,1)S(1)}, bf16[256,256]{1,0:T(8,128)(2,1)S(1)}, u32[]{:S(2)}, u32[]{:S(2)}) collective-permute-start(bf16[256,256]{1,0:T(8,128)(2,1)S(1)} %collective-permute-done), channel_id=1, source_target_pairs={{0,8},{8,0},{16,24},{24,16},{32,40},{40,32},{48,56},{56,48},{64,72... | collective-permute-start | bytes 393224 | tf_op jit(solution)/shard_map/ppermute | solution.py:81
  35.7 0.3 fusion.43
  36.0 0.2 fusion.83
  36.2 0.3 convolution_bitcast_fusion.10
  36.5 0.4 collective-permute-done.1
  37.0 0.4 fusion.35
  37.4 0.3 convolution_bitcast_fusion.5
  37.7 0.3 fusion.44
  38.0 0.4 fusion.27
  38.4 0.3 convolution_bitcast_fusion.7
  38.7 0.3 fusion.42
  39.0 0.3 convolution_bitcast_fusion.6
  39.3 4.2 %collective-permute-start.7 = (bf16[256,256]{1,0:T(8,128)(2,1)S(1)}, bf16[256,256]{1,0:T(8,128)(2,1)S(1)}, u32[]{:S(2)}, u32[]{:S(2)}) collective-permute-start(bf16[256,256]{1,0:T(8,128)(2,1)S(1)} %fusion.69), channel_id=1, source_target_pairs={{32,8},{48,24},{64,40},{80,56},{96,72},{112,88},{128,104},{144,120... | collective-permute-start | bytes 393224 | tf_op jit(solution)/shard_map/ppermute | solution.py:129
  43.5 0.3 convolution_bitcast_fusion.8
  43.9 1.9 %collective-permute-start.4 = (f32[256,256]{1,0:T(8,128)S(1)}, f32[256,256]{1,0:T(8,128)S(1)}, u32[]{:S(2)}, u32[]{:S(2)}) collective-permute-start(f32[256,256]{1,0:T(8,128)S(1)} %get-tuple-element.5), channel_id=1, source_target_pairs={{0,8},{8,0},{16,24},{24,16},{32,40},{40,32},{48,56},{56,48},{64,72... | collective-permute-start | bytes 786440 | tf_op jit(solution)/shard_map/ppermute | solution.py:126
  45.8 1.3 collective-permute-start.6
  47.1 0.3 fusion.45
  47.4 13.7 %collective-permute-start.5 = (bf16[256,256]{1,0:T(8,128)(2,1)S(1)}, bf16[256,256]{1,0:T(8,128)(2,1)S(1)}, u32[]{:S(2)}, u32[]{:S(2)}) collective-permute-start(bf16[256,256]{1,0:T(8,128)(2,1)S(1)} %fusion.65), channel_id=1, source_target_pairs={{16,0},{24,8},{32,16},{40,24},{48,32},{56,40},{64,48},{72,56},{80,... | collective-permute-start | bytes 393224 | tf_op jit(solution)/shard_map/ppermute | solution.py:13
  61.1 0.3 fusion.46
  61.4 3.7 %collective-permute-done.5 = bf16[256,256]{1,0:T(8,128)(2,1)S(1)} collective-permute-done((bf16[256,256]{1,0:T(8,128)(2,1)S(1)}, bf16[256,256]{1,0:T(8,128)(2,1)S(1)}, u32[]{:S(2)}, u32[]{:S(2)}) %collective-permute-start.5) | collective-permute-done | bytes 131104 | tf_op jit(solution)/shard_map/ppermute | solution.py:13
  65.2 0.1 copy.183
  65.3 1.3 fusion.40
  66.6 25.9 %all-to-all-start = ((bf16[64,8,768]{2,1,0:T(8,128)(2,1)}), bf16[64,8,768]{2,1,0:T(8,128)(2,1)S(1)}, u32[]{:S(2)}, u32[]{:S(2)}) async-start(bf16[64,8,768]{2,1,0:T(8,128)(2,1)} %fusion.40), calls=%async_computation | async-start | bytes 1572864 | tf_op jit(solution)/shard_map/all_to_all | solution.py:158
  92.6 0.6 reduce-window.24
  93.2 0.2 slice_reduce_fusion.1
  93.6 1.2 select_reduce_fusion
  94.8 0.1 eq.94
  94.9 1.2 fusion.59
  96.1 0.1 and.91
  96.2 33.7 %all-to-all-done = bf16[64,8,768]{2,1,0:T(8,128)(2,1)S(1)} async-done(((bf16[64,8,768]{2,1,0:T(8,128)(2,1)}), bf16[64,8,768]{2,1,0:T(8,128)(2,1)S(1)}, u32[]{:S(2)}, u32[]{:S(2)}) %all-to-all-start) | async-done | bytes 786464 | tf_op jit(solution)/shard_map/all_to_all | solution.py:158
  129.9 0.4 convolution_convert_fusion.1
  130.2 32.6 %all_to_all.28 = bf16[8,32,768]{2,1,0:T(8,128)(2,1)S(1)} all-to-all(bf16[8,32,768]{2,1,0:T(8,128)(2,1)S(1)} %bitcast.326), channel_id=1, replica_groups=mesh['ctx'=64,'head'=8] {'head'}, dimensions={0} | all-to-all | bytes 786432 | tf_op jit(solution)/shard_map/all_to_all | solution.py:176
  162.9 0.7 copy.227
  163.6 0.6 copy.235
  164.3 0.6 copy.236
  (38 shorter events, 0.7 us)
Async XLA Ops:
  0.6 29.1 %copy-start = (bf16[256,512]{1,0:T(8,128)(2,1)S(1)}, bf16[256,512]{1,0:T(8,128)(2,1)}, u32[]{:S(2)}) copy-start(bf16[256,512]{1,0:T(8,128)(2,1)} %param.12) | copy-start | bytes 786436
  0.6 29.2 %copy-start.3 = (bf16[256,512]{1,0:T(8,128)(2,1)S(1)}, bf16[256,512]{1,0:T(8,128)(2,1)}, u32[]{:S(2)}) copy-start(bf16[256,512]{1,0:T(8,128)(2,1)} %param.11) | copy-start | bytes 786436
  2.4 34.1 %collective-permute-start.3 = (bf16[256,256]{1,0:T(8,128)(2,1)S(1)}, bf16[256,256]{1,0:T(8,128)(2,1)S(1)}, u32[]{:S(2)}, u32[]{:S(2)}) collective-permute-start(bf16[256,256]{1,0:T(8,128)(2,1)S(1)} %constant_dynamic-update-slice_fusion), channel_id=1, source_target_pairs={{8,32},{24,48},{40,64},{56,80},{72,96},{88,112},{104,128},{120,144... | collective-permute-start | bytes 393224 | tf_op jit(solution)/shard_map/ppermute | solution.py:82
  3.7 32.8 %collective-permute-start.2 = (bf16[256,256]{1,0:T(8,128)(2,1)S(1)}, bf16[256,256]{1,0:T(8,128)(2,1)S(1)}, u32[]{:S(2)}, u32[]{:S(2)}) collective-permute-start(bf16[256,256]{1,0:T(8,128)(2,1)S(1)} %constant_dynamic-update-slice_fusion), channel_id=1, source_target_pairs={{0,8},{16,24},{32,40},{48,56},{64,72},{80,88},{96,104},{112,120},{... | collective-permute-start | bytes 393224 | tf_op jit(solution)/shard_map/ppermute | solution.py:80
  8.0 25.1 %collective-permute-start = (bf16[256,256]{1,0:T(8,128)(2,1)S(1)}, bf16[256,256]{1,0:T(8,128)(2,1)S(1)}, u32[]{:S(2)}, u32[]{:S(2)}) collective-permute-start(bf16[256,256]{1,0:T(8,128)(2,1)S(1)} %constant_dynamic-update-slice_fusion), channel_id=1, source_target_pairs={{0,16},{8,24},{16,32},{24,40},{32,48},{40,56},{48,64},{56,72},{64,... | collective-permute-start | bytes 393224 | tf_op jit(solution)/shard_map/ppermute | solution.py:13
  29.9 1.0 copy-start.2
  29.9 1.0 copy-start.5
  31.3 0.8 copy-start.4
  33.7 3.2 %collective-permute-start.1 = (bf16[256,256]{1,0:T(8,128)(2,1)S(1)}, bf16[256,256]{1,0:T(8,128)(2,1)S(1)}, u32[]{:S(2)}, u32[]{:S(2)}) collective-permute-start(bf16[256,256]{1,0:T(8,128)(2,1)S(1)} %collective-permute-done), channel_id=1, source_target_pairs={{0,8},{8,0},{16,24},{24,16},{32,40},{40,32},{48,56},{56,48},{64,72... | collective-permute-start | bytes 393224 | tf_op jit(solution)/shard_map/ppermute | solution.py:81
  39.3 22.1 %collective-permute-start.7 = (bf16[256,256]{1,0:T(8,128)(2,1)S(1)}, bf16[256,256]{1,0:T(8,128)(2,1)S(1)}, u32[]{:S(2)}, u32[]{:S(2)}) collective-permute-start(bf16[256,256]{1,0:T(8,128)(2,1)S(1)} %fusion.69), channel_id=1, source_target_pairs={{32,8},{48,24},{64,40},{80,56},{96,72},{112,88},{128,104},{144,120... | collective-permute-start | bytes 393224 | tf_op jit(solution)/shard_map/ppermute | solution.py:129
  43.9 3.5 %collective-permute-start.4 = (f32[256,256]{1,0:T(8,128)S(1)}, f32[256,256]{1,0:T(8,128)S(1)}, u32[]{:S(2)}, u32[]{:S(2)}) collective-permute-start(f32[256,256]{1,0:T(8,128)S(1)} %get-tuple-element.5), channel_id=1, source_target_pairs={{0,8},{8,0},{16,24},{24,16},{32,40},{40,32},{48,56},{56,48},{64,72... | collective-permute-start | bytes 786440 | tf_op jit(solution)/shard_map/ppermute | solution.py:126
  45.8 15.6 %collective-permute-start.6 = (f32[256,256]{1,0:T(8,128)S(1)}, f32[256,256]{1,0:T(8,128)S(1)}, u32[]{:S(2)}, u32[]{:S(2)}) collective-permute-start(f32[256,256]{1,0:T(8,128)S(1)} %get-tuple-element.6), channel_id=1, source_target_pairs={{8,0},{24,16},{40,32},{56,48},{72,64},{88,80},{104,96},{120,112},{... | collective-permute-start | bytes 786440 | tf_op jit(solution)/shard_map/ppermute | solution.py:127
  47.4 17.7 %collective-permute-start.5 = (bf16[256,256]{1,0:T(8,128)(2,1)S(1)}, bf16[256,256]{1,0:T(8,128)(2,1)S(1)}, u32[]{:S(2)}, u32[]{:S(2)}) collective-permute-start(bf16[256,256]{1,0:T(8,128)(2,1)S(1)} %fusion.65), channel_id=1, source_target_pairs={{16,0},{24,8},{32,16},{40,24},{48,32},{56,40},{64,48},{72,56},{80,... | collective-permute-start | bytes 393224 | tf_op jit(solution)/shard_map/ppermute | solution.py:13
  66.6 25.9 %copy-start.1 = (s32[16384]{0:T(1024)S(1)}, s32[16384]{0:T(1024)}, u32[]{:S(2)}) copy-start(s32[16384]{0:T(1024)} %param.15) | copy-start | bytes 196612
  66.6 63.3 %all-to-all-start = ((bf16[64,8,768]{2,1,0:T(8,128)(2,1)}), bf16[64,8,768]{2,1,0:T(8,128)(2,1)S(1)}, u32[]{:S(2)}, u32[]{:S(2)}) async-start(bf16[64,8,768]{2,1,0:T(8,128)(2,1)} %fusion.40), calls=%async_computation | async-start | bytes 1572864 | tf_op jit(solution)/shard_map/all_to_all | solution.py:158

commit v4 on v3

--- a/solution.py
+++ b/solution.py
@@ -77,60 +77,65 @@
     even = block_index % 2 == 0
     partner = [(i, i ^ 1) for i in range(blocks)]
     kv_two = from_behind(kv_own, "ctx", 2)
-    kv_partner_own = lax.ppermute(kv_own, "ctx", [(i, i + 1) for i in range(0, blocks, 2)])
-    kv_partner_two = lax.ppermute(kv_two, "ctx", partner)
     kv_three = lax.ppermute(
         kv_own, "ctx", [(i, i + 3) for i in range(1, blocks, 2) if i + 3 < blocks]
     )
-    kv_behind = [
-        jnp.where(even, kv_partner_two, kv_partner_own),
-        kv_two,
-        jnp.where(even, kv_three, kv_partner_two),
-    ]
-
-    query_pos = block_index * length + lax.iota(jnp.int32, length)
-    finish = jnp.cumsum(document_lengths)
-    firsts = finish - document_lengths
-    begins = jnp.max(jnp.where(firsts[None, :] <= query_pos[:, None], firsts[None, :], 0), axis=1)
-    query_vectors = query_head_rows.reshape(length, kv_heads, query_groups, HEAD_SIZE)
-    output_gradient = cotangent.reshape(length, kv_heads, query_groups, HEAD_SIZE)
-    log_normalizer = logsumexp.T.reshape(length, kv_heads, query_groups)
+
+    def query_side(index, rows_q, rows_do, lse, correction):
+        positions = index * length + lax.iota(jnp.int32, length)
+        finish = jnp.cumsum(document_lengths)
+        firsts = finish - document_lengths
+        starts = jnp.max(
+            jnp.where(firsts[None, :] <= positions[:, None], firsts[None, :], 0), axis=1
+        )
+        return (
+            rows_q.reshape(length, kv_heads, query_groups, HEAD_SIZE),
+            rows_do.reshape(length, kv_heads, query_groups, HEAD_SIZE),
+            lse.T.reshape(length, kv_heads, query_groups),
+            correction,
+            starts,
+            positions,
+        )
+
     row_correction = jnp.sum(
-        output_gradient.astype(jnp.float32)
+        cotangent.reshape(length, kv_heads, query_groups, HEAD_SIZE).astype(jnp.float32)
         * forward_output.reshape(length, kv_heads, query_groups, HEAD_SIZE).astype(jnp.float32),
         axis=3,
     )
-
-    def block_terms(kv_part, distance):
-        key_start = (block_index - distance) * length
+    mine = query_side(block_index, query_head_rows, cotangent, logsumexp, row_correction)
+    theirs_rows = lax.ppermute(
+        (query_head_rows, cotangent, logsumexp, row_correction), "ctx", partner
+    )
+    theirs = query_side(block_index ^ 1, *theirs_rows)
+
+    def block_terms(side, kv_part, key_block):
         key_heads = kv_part[:, :kv_width].reshape(length, kv_heads, HEAD_SIZE)
         value_heads = kv_part[:, kv_width:].reshape(length, kv_heads, HEAD_SIZE)
-        return block_grads(
-            query_vectors,
-            output_gradient,
-            log_normalizer,
-            row_correction,
-            begins,
-            query_pos,
-            key_heads,
-            value_heads,
-            key_start,
+        query_term, key_term, value_term = block_grads(
+            *side, key_heads, value_heads, key_block * length
         )
-
-    query_acc, key_sum, value_sum = block_terms(kv_own, 0)
-    partials = []
-    for distance in range(1, DOC_BLOCKS + 1):
-        query_term, key_term, value_term = block_terms(kv_behind[distance - 1], distance)
-        query_acc = query_acc + query_term
-        partials.append(jnp.concatenate([key_term, value_term], axis=1))
-    swapped = lax.ppermute(jnp.where(even, partials[0], partials[2]), "ctx", partner)
-    to_partner = lax.ppermute(partials[0], "ctx", [(i, i - 1) for i in range(1, blocks, 2)])
-    crossed = from_behind((partials[1] + swapped).astype(jnp.bfloat16), "ctx", -2)
+        return query_term, jnp.concatenate([key_term, value_term], axis=1)
+
+    q_own, kv_grad_own = block_terms(mine, kv_own, block_index)
+    q_two, kv_grad_two = block_terms(mine, kv_two, block_index - 2)
+    q_cross, kv_grad_cross = block_terms(theirs, kv_two, block_index - 2)
+    q_three, kv_grad_three = block_terms(mine, kv_three, block_index - 3)
+    q_next, kv_grad_next = block_terms(theirs, kv_own, block_index)
+
+    zero_q = jnp.zeros_like(q_own)
+    zero_kv = jnp.zeros_like(kv_grad_own)
+    sent_q = q_cross + jnp.where(even, q_next, zero_q)
+    back_q = lax.ppermute(sent_q, "ctx", partner)
+    query_acc = q_own + q_two + jnp.where(even, q_three, zero_q) + back_q
+
+    crossed = from_behind((kv_grad_two + kv_grad_cross).astype(jnp.bfloat16), "ctx", -2)
     from_three = lax.ppermute(
-        partials[2].astype(jnp.bfloat16), "ctx", [(i, i - 3) for i in range(0, blocks, 2) if i >= 3]
-    )
-    own_sum = jnp.concatenate([key_sum, value_sum], axis=1) + crossed.astype(jnp.float32)
-    own_sum = own_sum + jnp.where(even, to_partner, from_three.astype(jnp.float32))
+        kv_grad_three.astype(jnp.bfloat16),
+        "ctx",
+        [(i, i - 3) for i in range(0, blocks, 2) if i >= 3],
+    )
+    own_sum = kv_grad_own + crossed.astype(jnp.float32)
+    own_sum = own_sum + jnp.where(even, kv_grad_next, from_three.astype(jnp.float32))
     key_sum = own_sum[:, :kv_width]
     value_sum = own_sum[:, kv_width:]
 

time: 166 us -> 159 us (0.958)
  starting transfers between devices: 70.2 us -> 45.1 us
  blocking collectives: 32.6 us -> 56.7 us
  waiting for transfers between devices: 37.9 us -> 32.8 us
  other arithmetic: 8.1 us -> 6.42 us
    all_to_all x1, blocking collectives: 32.6 us -> 56.7 us  [per_device(): lax.all_to_all(linear_rows, 'head', split_axis=0, concat_axis=1, tiled=True)]
    all_to_all x1, starting transfers between devices: 25.9 us -> 8.41 us  [per_device(): lax.all_to_all(packed, 'ctx', split_axis=0, concat_axis=0, tiled=True)]
    all_to_all x1, waiting for transfers between devices: 33.7 us -> 19.6 us  [per_device(): lax.all_to_all(packed, 'ctx', split_axis=0, concat_axis=0, tiled=True)]
    ppermute x2, starting transfers between devices: 29.4 us -> 18.7 us  [from_behind(): return lax.ppermute(shard, axis, pairs)]
    ppermute x2, waiting for transfers between devices: 3.72 us -> 13.2 us  [from_behind(): return lax.ppermute(shard, axis, pairs)]
    ppermute x5 -> x6, starting transfers between devices: 13.6 us -> 16.7 us  [the longest x4 10.2 us: per_device(): lax.ppermute((query_head_rows, cotangent, logsumexp, row_correction), 'ct...]
  transfers between devices with their start and end apart: 9 -> 10, of which waited for: 3 -> 2; matrix products, arithmetic and copies ran while one was open for 9% -> 10% of each run, Pallas kernels for 0% -> 0%
where the time goes in v4:
time: 159 us; the launch traced here: 158 us
  blocking collectives  56.7 us (36%)
  starting transfers between devices  45.1 us (28%)
  waiting for transfers between devices  32.8 us (21%)
  matrix products  9.32 us (6%)
  local copies, waits for them, and re-layouts  6.54 us (4%)
  other arithmetic  6.42 us (4%)
    all_to_all x1, blocking collectives, per_device(): lax.all_to_all(linear_rows, 'head', split_axis=0, concat_axis=1, tiled=True)  56.7 us
    all_to_all x1, waiting for transfers between devices, per_device(): lax.all_to_all(packed, 'ctx', split_axis=0, concat_axis=0, tiled=True)  19.6 us
    ppermute x2, starting transfers between devices, from_behind(): return lax.ppermute(shard, axis, pairs)  18.7 us
    ppermute x2, waiting for transfers between devices, from_behind(): return lax.ppermute(shard, axis, pairs)  13.2 us
    ppermute x4, starting transfers between devices, per_device(): lax.ppermute((query_head_rows, cotangent, logsumexp, row_correction), 'ct...  10.2 us
    all_to_all x1, starting transfers between devices, per_device(): lax.all_to_all(packed, 'ctx', split_axis=0, concat_axis=0, tiled=True)  8.41 us
    ppermute x1, starting transfers between devices, per_device(): lax.ppermute(kv_grad_three.astype(jnp.bfloat16), 'ctx', [(i, i - 3) for i...  4.57 us
  transfers between devices with their start and end apart: 10, of which 2 were waited for; matrix products, arithmetic and copies ran while one was open for 10% of the time, Pallas kernels for 0%

profile of v4, /device:TPU:2, one launch (start us, length us, event | category | flops | bytes accessed | tf_op | source)
XLA Modules:
  0.0 158.1 jit_solution(8468780717058738706)
XLA Ops:
  0.6 0.9 constant_dynamic-update-slice_fusion.1
  1.5 0.9 constant_dynamic-update-slice_fusion
  2.3 1.3 collective-permute-start.1
  3.6 15.7 %collective-permute-start = (bf16[256,256]{1,0:T(8,128)(2,1)S(1)}, bf16[256,256]{1,0:T(8,128)(2,1)S(1)}, u32[]{:S(2)}, u32[]{:S(2)}) collective-permute-start(bf16[256,256]{1,0:T(8,128)(2,1)S(1)} %constant_dynamic-update-slice_fusion), channel_id=1, source_target_pairs={{0,16},{8,24},{16,32},{24,40},{32,48},{40,56},{48,64},{56,72},{64,... | collective-permute-start | bytes 393224 | tf_op jit(solution)/shard_map/ppermute | solution.py:13
  19.4 3.9 %collective-permute-start.3 = (f32[4,256]{1,0:T(4,128)}, f32[4,256]{1,0:T(4,128)S(1)}, u32[]{:S(2)}, u32[]{:S(2)}) collective-permute-start(f32[4,256]{1,0:T(4,128)} %param.13), channel_id=1, source_target_pairs={{0,8},{8,0},{16,24},{24,16},{32,40},{40,32},{48,56},{56,48},{64,72... | collective-permute-start | bytes 12296 | tf_op jit(solution)/shard_map/ppermute | solution.py:106
  23.3 1.1 copy.192
  24.4 1.9 %collective-permute-start.4 = (bf16[256,512]{0,1:T(8,128)(2,1)S(1)}, bf16[256,512]{0,1:T(8,128)(2,1)S(1)}, u32[]{:S(2)}, u32[]{:S(2)}) collective-permute-start(bf16[256,512]{0,1:T(8,128)(2,1)S(1)} %copy.192), channel_id=1, source_target_pairs={{0,8},{8,0},{16,24},{24,16},{32,40},{40,32},{48,56},{56,48},{64,72... | collective-permute-start | bytes 786440 | tf_op jit(solution)/shard_map/ppermute | solution.py:106
  26.3 1.1 convert_multiply_fusion
  27.5 0.2 mul.108
  27.7 0.3 reduce_sum.31
  28.1 2.4 %collective-permute-start.5 = (f32[256,1,4]{2,0,1:T(8,128)S(1)}, f32[256,1,4]{2,0,1:T(8,128)S(1)}, u32[]{:S(2)}, u32[]{:S(2)}) collective-permute-start(f32[256,1,4]{2,0,1:T(8,128)S(1)} %bitcast.406), channel_id=1, source_target_pairs={{0,8},{8,0},{16,24},{24,16},{32,40},{40,32},{48,56},{56,48},{64,72... | collective-permute-start | bytes 12296 | tf_op jit(solution)/shard_map/ppermute | solution.py:106
  30.7 0.1 copy.119
  30.8 0.1 reduce-window.33
  30.9 0.1 reduce.4
  31.1 0.6 reduce-window.31
  31.7 0.2 slice_reduce_fusion
  31.9 0.1 fusion.92
  32.1 0.1 copy.191
  32.3 0.1 select_reduce_fusion.1
  32.4 0.3 compare_and_fusion.1
  32.7 0.4 fusion.28
  33.1 0.3 convolution_bitcast_fusion.14
  33.4 0.5 copy-done.1
  33.9 0.3 fusion.51
  34.2 0.3 convolution_bitcast_fusion.5
  34.5 0.3 convolution_bitcast_fusion.15
  34.8 1.9 %collective-permute-start.2 = (bf16[256,512]{0,1:T(8,128)(2,1)S(1)}, bf16[256,512]{0,1:T(8,128)(2,1)S(1)}, u32[]{:S(2)}, u32[]{:S(2)}) collective-permute-start(bf16[256,512]{0,1:T(8,128)(2,1)S(1)} %copy.191), channel_id=1, source_target_pairs={{0,8},{8,0},{16,24},{24,16},{32,40},{40,32},{48,56},{56,48},{64,72... | collective-permute-start | bytes 786440 | tf_op jit(solution)/shard_map/ppermute | solution.py:106
  36.8 0.4 fusion.36
  37.2 0.3 fusion.63
  37.5 0.3 fusion.53
  37.8 0.3 fusion.62
  38.2 4.6 %collective-permute-start.8 = (bf16[256,256]{0,1:T(8,128)(2,1)S(1)}, bf16[256,256]{0,1:T(8,128)(2,1)S(1)}, u32[]{:S(2)}, u32[]{:S(2)}) collective-permute-start(bf16[256,256]{0,1:T(8,128)(2,1)S(1)} %pad_maximum_fusion), channel_id=1, source_target_pairs={{32,8},{48,24},{64,40},{80,56},{96,72},{112,88},{128,104},{144,120... | collective-permute-start | bytes 393224 | tf_op jit(solution)/shard_map/ppermute | solution.py:132
  42.7 0.2 convolution_select_fusion.1
  43.0 0.4 fusion.32
  43.4 0.3 fusion.52
  43.7 0.3 convolution_bitcast_fusion.12
  44.0 0.3 convolution_bitcast_fusion.13
  44.3 0.4 fusion.40
  44.7 0.3 convolution_bitcast_fusion.10
  45.0 0.3 fusion.54
  45.3 0.3 convolution_bitcast_fusion.11
  45.6 0.4 fusion.44
  46.0 0.3 fusion.55
  46.3 0.3 fusion.56
  46.6 0.3 fusion.57
  46.8 1.9 %collective-permute-start.6 = (f32[256,1,4,128]{0,3,2,1:T(8,128)S(1)}, f32[256,1,4,128]{0,3,2,1:T(8,128)S(1)}, u32[]{:S(2)}, u32[]{:S(2)}) collective-permute-start(f32[256,1,4,128]{0,3,2,1:T(8,128)S(1)} %fusion.57), channel_id=1, source_target_pairs={{0,8},{8,0},{16,24},{24,16},{32,40},{40,32},{48,56},{56,48},{64,72... | collective-permute-start | bytes 1572872 | tf_op jit(solution)/shard_map/ppermute | solution.py:128
  48.8 3.0 %collective-permute-start.7 = (bf16[256,256]{0,1:T(8,128)(2,1)S(1)}, bf16[256,256]{0,1:T(8,128)(2,1)S(1)}, u32[]{:S(2)}, u32[]{:S(2)}) collective-permute-start(bf16[256,256]{0,1:T(8,128)(2,1)S(1)} %fusion.84), channel_id=1, source_target_pairs={{16,0},{24,8},{32,16},{40,24},{48,32},{56,40},{64,48},{72,56},{80,... | collective-permute-start | bytes 393224 | tf_op jit(solution)/shard_map/ppermute | solution.py:13
  51.8 0.3 convolution_bitcast_fusion.8
  52.1 0.3 convolution_bitcast_fusion.9
  52.5 13.2 %collective-permute-done.7 = bf16[256,256]{0,1:T(8,128)(2,1)S(1)} collective-permute-done((bf16[256,256]{0,1:T(8,128)(2,1)S(1)}, bf16[256,256]{0,1:T(8,128)(2,1)S(1)}, u32[]{:S(2)}, u32[]{:S(2)}) %collective-permute-start.7) | collective-permute-done | bytes 131104 | tf_op jit(solution)/shard_map/ppermute | solution.py:13
  65.8 0.3 fusion.61
  66.0 1.3 fusion.50
  67.3 8.4 %all-to-all-start = ((bf16[64,8,768]{2,1,0:T(8,128)(2,1)}), bf16[64,8,768]{2,1,0:T(8,128)(2,1)S(1)}, u32[]{:S(2)}, u32[]{:S(2)}) async-start(bf16[64,8,768]{2,1,0:T(8,128)(2,1)} %fusion.50), calls=%async_computation | async-start | bytes 1572864 | tf_op jit(solution)/shard_map/all_to_all | solution.py:163
  75.8 0.6 reduce-window.24
  76.4 0.2 slice_reduce_fusion.1
  76.9 1.2 select_reduce_fusion
  78.1 1.2 fusion.78
  79.3 0.1 and.98
  79.4 19.6 %all-to-all-done = bf16[64,8,768]{2,1,0:T(8,128)(2,1)S(1)} async-done(((bf16[64,8,768]{2,1,0:T(8,128)(2,1)}), bf16[64,8,768]{2,1,0:T(8,128)(2,1)S(1)}, u32[]{:S(2)}, u32[]{:S(2)}) %all-to-all-start) | async-done | bytes 786464 | tf_op jit(solution)/shard_map/all_to_all | solution.py:163
  99.0 0.4 convolution_convert_fusion.1
  99.4 56.7 %all_to_all.28 = bf16[8,32,768]{2,1,0:T(8,128)(2,1)S(1)} all-to-all(bf16[8,32,768]{2,1,0:T(8,128)(2,1)S(1)} %bitcast.407), channel_id=1, replica_groups=mesh['ctx'=64,'head'=8] {'head'}, dimensions={0} | all-to-all | bytes 786432 | tf_op jit(solution)/shard_map/all_to_all | solution.py:181
  156.1 0.7 copy.195
  156.9 0.6 copy.203
  157.5 0.6 copy.204
  (43 shorter events, 1.0 us)
Async XLA Ops:
  2.3 34.5 %collective-permute-start.1 = (bf16[256,256]{1,0:T(8,128)(2,1)S(1)}, bf16[256,256]{1,0:T(8,128)(2,1)S(1)}, u32[]{:S(2)}, u32[]{:S(2)}) collective-permute-start(bf16[256,256]{1,0:T(8,128)(2,1)S(1)} %constant_dynamic-update-slice_fusion), channel_id=1, source_target_pairs={{8,32},{24,48},{40,64},{56,80},{72,96},{88,112},{104,128},{120,144... | collective-permute-start | bytes 393224 | tf_op jit(solution)/shard_map/ppermute | solution.py:80
  3.6 39.4 %collective-permute-start = (bf16[256,256]{1,0:T(8,128)(2,1)S(1)}, bf16[256,256]{1,0:T(8,128)(2,1)S(1)}, u32[]{:S(2)}, u32[]{:S(2)}) collective-permute-start(bf16[256,256]{1,0:T(8,128)(2,1)S(1)} %constant_dynamic-update-slice_fusion), channel_id=1, source_target_pairs={{0,16},{8,24},{16,32},{24,40},{32,48},{40,56},{48,64},{56,72},{64,... | collective-permute-start | bytes 393224 | tf_op jit(solution)/shard_map/ppermute | solution.py:13
  19.4 24.9 %collective-permute-start.3 = (f32[4,256]{1,0:T(4,128)}, f32[4,256]{1,0:T(4,128)S(1)}, u32[]{:S(2)}, u32[]{:S(2)}) collective-permute-start(f32[4,256]{1,0:T(4,128)} %param.13), channel_id=1, source_target_pairs={{0,8},{8,0},{16,24},{24,16},{32,40},{40,32},{48,56},{56,48},{64,72... | collective-permute-start | bytes 12296 | tf_op jit(solution)/shard_map/ppermute | solution.py:106
  24.4 20.3 %collective-permute-start.4 = (bf16[256,512]{0,1:T(8,128)(2,1)S(1)}, bf16[256,512]{0,1:T(8,128)(2,1)S(1)}, u32[]{:S(2)}, u32[]{:S(2)}) collective-permute-start(bf16[256,512]{0,1:T(8,128)(2,1)S(1)} %copy.192), channel_id=1, source_target_pairs={{0,8},{8,0},{16,24},{24,16},{32,40},{40,32},{48,56},{56,48},{64,72... | collective-permute-start | bytes 786440 | tf_op jit(solution)/shard_map/ppermute | solution.py:106
  27.5 3.0 %copy-start.2 = (s32[16384]{0:T(1024)S(1)}, s32[16384]{0:T(1024)}, u32[]{:S(2)}) copy-start(s32[16384]{0:T(1024)} %param.15) | copy-start | bytes 196612
  27.5 3.3 %copy-start.4 = (s32[64]{0:T(128)S(1)}, s32[64]{0:T(128)}, u32[]{:S(2)}) copy-start(s32[64]{0:T(128)} %param.14) | copy-start | bytes 772
  27.5 4.6 %copy-start.3 = (bf16[256,512]{1,0:T(8,128)(2,1)S(1)}, bf16[256,512]{1,0:T(8,128)(2,1)}, u32[]{:S(2)}) copy-start(bf16[256,512]{1,0:T(8,128)(2,1)} %param.8) | copy-start | bytes 786436
  27.7 5.0 %copy-start = (bf16[256,128]{1,0:T(8,128)(2,1)S(1)}, bf16[256,128]{1,0:T(8,128)(2,1)}, u32[]{:S(2)}) copy-start(bf16[256,128]{1,0:T(8,128)(2,1)} %param.9) | copy-start | bytes 196612
  27.7 5.0 %copy-start.5 = (f32[4,256]{1,0:T(4,128)S(1)}, f32[4,256]{1,0:T(4,128)}, u32[]{:S(2)}) copy-start(f32[4,256]{1,0:T(4,128)} %param.13) | copy-start | bytes 12292
  28.1 6.8 %collective-permute-start.5 = (f32[256,1,4]{2,0,1:T(8,128)S(1)}, f32[256,1,4]{2,0,1:T(8,128)S(1)}, u32[]{:S(2)}, u32[]{:S(2)}) collective-permute-start(f32[256,1,4]{2,0,1:T(8,128)S(1)} %bitcast.406), channel_id=1, source_target_pairs={{0,8},{8,0},{16,24},{24,16},{32,40},{40,32},{48,56},{56,48},{64,72... | collective-permute-start | bytes 12296 | tf_op jit(solution)/shard_map/ppermute | solution.py:106
  33.1 0.8 copy-start.1
  34.8 9.5 %collective-permute-start.2 = (bf16[256,512]{0,1:T(8,128)(2,1)S(1)}, bf16[256,512]{0,1:T(8,128)(2,1)S(1)}, u32[]{:S(2)}, u32[]{:S(2)}) collective-permute-start(bf16[256,512]{0,1:T(8,128)(2,1)S(1)} %copy.191), channel_id=1, source_target_pairs={{0,8},{8,0},{16,24},{24,16},{32,40},{40,32},{48,56},{56,48},{64,72... | collective-permute-start | bytes 786440 | tf_op jit(solution)/shard_map/ppermute | solution.py:106
  38.2 14.3 %collective-permute-start.8 = (bf16[256,256]{0,1:T(8,128)(2,1)S(1)}, bf16[256,256]{0,1:T(8,128)(2,1)S(1)}, u32[]{:S(2)}, u32[]{:S(2)}) collective-permute-start(bf16[256,256]{0,1:T(8,128)(2,1)S(1)} %pad_maximum_fusion), channel_id=1, source_target_pairs={{32,8},{48,24},{64,40},{80,56},{96,72},{112,88},{128,104},{144,120... | collective-permute-start | bytes 393224 | tf_op jit(solution)/shard_map/ppermute | solution.py:132
  46.8 18.9 %collective-permute-start.6 = (f32[256,1,4,128]{0,3,2,1:T(8,128)S(1)}, f32[256,1,4,128]{0,3,2,1:T(8,128)S(1)}, u32[]{:S(2)}, u32[]{:S(2)}) collective-permute-start(f32[256,1,4,128]{0,3,2,1:T(8,128)S(1)} %fusion.57), channel_id=1, source_target_pairs={{0,8},{8,0},{16,24},{24,16},{32,40},{40,32},{48,56},{56,48},{64,72... | collective-permute-start | bytes 1572872 | tf_op jit(solution)/shard_map/ppermute | solution.py:128
  48.8 16.9 %collective-permute-start.7 = (bf16[256,256]{0,1:T(8,128)(2,1)S(1)}, bf16[256,256]{0,1:T(8,128)(2,1)S(1)}, u32[]{:S(2)}, u32[]{:S(2)}) collective-permute-start(bf16[256,256]{0,1:T(8,128)(2,1)S(1)} %fusion.84), channel_id=1, source_target_pairs={{16,0},{24,8},{32,16},{40,24},{48,32},{56,40},{64,48},{72,56},{80,... | collective-permute-start | bytes 393224 | tf_op jit(solution)/shard_map/ppermute | solution.py:13
  67.3 31.6 %all-to-all-start = ((bf16[64,8,768]{2,1,0:T(8,128)(2,1)}), bf16[64,8,768]{2,1,0:T(8,128)(2,1)S(1)}, u32[]{:S(2)}, u32[]{:S(2)}) async-start(bf16[64,8,768]{2,1,0:T(8,128)(2,1)} %fusion.50), calls=%async_computation | async-start | bytes 1572864 | tf_op jit(solution)/shard_map/all_to_all | solution.py:163

commit v5 on v4

--- a/solution.py
+++ b/solution.py
@@ -3,8 +3,8 @@
 from jax import lax
 from jax.sharding import PartitionSpec as P
 
+
 HEAD_SIZE = 128
-DOC_BLOCKS = 3
 
 
 def from_behind(shard, axis, by):
@@ -103,10 +103,20 @@
         axis=3,
     )
     mine = query_side(block_index, query_head_rows, cotangent, logsumexp, row_correction)
-    theirs_rows = lax.ppermute(
-        (query_head_rows, cotangent, logsumexp, row_correction), "ctx", partner
-    )
-    theirs = query_side(block_index ^ 1, *theirs_rows)
+    their_q = lax.ppermute(query_head_rows, "ctx", partner)
+    their_do = lax.ppermute(cotangent, "ctx", partner)
+    their_high = lax.ppermute(
+        jnp.concatenate([logsumexp, row_correction.reshape(length, -1).T], axis=0),
+        "ctx",
+        partner,
+    )
+    theirs = query_side(
+        block_index ^ 1,
+        their_q,
+        their_do,
+        their_high[: logsumexp.shape[0]],
+        their_high[logsumexp.shape[0] :].T.reshape(row_correction.shape),
+    )
 
     def block_terms(side, kv_part, key_block):
         key_heads = kv_part[:, :kv_width].reshape(length, kv_heads, HEAD_SIZE)

time: 159 us -> 155 us (0.975)
  blocking collectives: 56.7 us -> 37 us
  starting transfers between devices: 45.1 us -> 56.3 us
  waiting for transfers between devices: 32.8 us -> 37.5 us
    all_to_all x1, blocking collectives: 56.7 us -> 37 us  [per_device(): lax.all_to_all(linear_rows, 'head', split_axis=0, concat_axis=1, tiled=True)]
    all_to_all x1, starting transfers between devices: 8.41 us -> 15.7 us  [per_device(): lax.all_to_all(packed, 'ctx', split_axis=0, concat_axis=0, tiled=True)]
    ppermute x2, starting transfers between devices: 18.7 us -> 25.1 us  [from_behind(): return lax.ppermute(shard, axis, pairs)]
    all_to_all x1, waiting for transfers between devices: 19.6 us -> 25.2 us  [per_device(): lax.all_to_all(packed, 'ctx', split_axis=0, concat_axis=0, tiled=True)]
    ppermute x4 -> x3, starting transfers between devices: 10.2 us -> 8.26 us  [the longest x1 3.94 us: per_device(): their_do = lax.ppermute(cotangent, 'ctx', partner)]
  transfers between devices with their start and end apart: 10 -> 9, of which waited for: 2 -> 2; matrix products, arithmetic and copies ran while one was open for 10% -> 10% of each run, Pallas kernels for 0% -> 0%
where the time goes in v5:
time: 155 us; the launch traced here: 154 us
  starting transfers between devices  56.3 us (36%)
  waiting for transfers between devices  37.5 us (24%)
  blocking collectives  37 us (24%)
  matrix products  9.31 us (6%)
  local copies, waits for them, and re-layouts  7.58 us (5%)
  other arithmetic  5.38 us (3%)
    all_to_all x1, blocking collectives, per_device(): lax.all_to_all(linear_rows, 'head', split_axis=0, concat_axis=1, tiled=True)  37 us
    all_to_all x1, waiting for transfers between devices, per_device(): lax.all_to_all(packed, 'ctx', split_axis=0, concat_axis=0, tiled=True)  25.2 us
    ppermute x2, starting transfers between devices, from_behind(): return lax.ppermute(shard, axis, pairs)  25.1 us
    all_to_all x1, starting transfers between devices, per_device(): lax.all_to_all(packed, 'ctx', split_axis=0, concat_axis=0, tiled=True)  15.7 us
    ppermute x2, waiting for transfers between devices, from_behind(): return lax.ppermute(shard, axis, pairs)  12.3 us
    ppermute x1, starting transfers between devices, per_device(): lax.ppermute(kv_grad_three.astype(jnp.bfloat16), 'ctx', [(i, i - 3) for i...  4.08 us
    ppermute x1, starting transfers between devices, per_device(): their_do = lax.ppermute(cotangent, 'ctx', partner)  3.94 us
  transfers between devices with their start and end apart: 9, of which 2 were waited for; matrix products, arithmetic and copies ran while one was open for 10% of the time, Pallas kernels for 0%

profile of v5, /device:TPU:2, one launch (start us, length us, event | category | flops | bytes accessed | tf_op | source)
XLA Modules:
  0.0 154.3 jit_solution(7867173710198713034)
XLA Ops:
  0.7 0.9 constant_dynamic-update-slice_fusion.1
  1.6 0.9 constant_dynamic-update-slice_fusion
  2.4 1.3 collective-permute-start.1
  3.7 15.7 %collective-permute-start = (bf16[256,256]{1,0:T(8,128)(2,1)S(1)}, bf16[256,256]{1,0:T(8,128)(2,1)S(1)}, u32[]{:S(2)}, u32[]{:S(2)}) collective-permute-start(bf16[256,256]{1,0:T(8,128)(2,1)S(1)} %constant_dynamic-update-slice_fusion), channel_id=1, source_target_pairs={{0,16},{8,24},{16,32},{24,40},{32,48},{40,56},{48,64},{56,72},{64,... | collective-permute-start | bytes 393224 | tf_op jit(solution)/shard_map/ppermute | solution.py:13
  19.5 1.1 copy.244
  20.5 3.9 %collective-permute-start.4 = (bf16[256,512]{0,1:T(8,128)(2,1)S(1)}, bf16[256,512]{0,1:T(8,128)(2,1)S(1)}, u32[]{:S(2)}, u32[]{:S(2)}) collective-permute-start(bf16[256,512]{0,1:T(8,128)(2,1)S(1)} %copy.244), channel_id=1, source_target_pairs={{0,8},{8,0},{16,24},{24,16},{32,40},{40,32},{48,56},{56,48},{64,72... | collective-permute-start | bytes 786440 | tf_op jit(solution)/shard_map/ppermute | solution.py:107
  24.5 1.1 copy.243
  25.6 1.9 %collective-permute-start.2 = (bf16[256,512]{0,1:T(8,128)(2,1)S(1)}, bf16[256,512]{0,1:T(8,128)(2,1)S(1)}, u32[]{:S(2)}, u32[]{:S(2)}) collective-permute-start(bf16[256,512]{0,1:T(8,128)(2,1)S(1)} %copy.243), channel_id=1, source_target_pairs={{0,8},{8,0},{16,24},{24,16},{32,40},{40,32},{48,56},{56,48},{64,72... | collective-permute-start | bytes 786440 | tf_op jit(solution)/shard_map/ppermute | solution.py:106
  27.6 0.2 mul.108
  27.8 0.3 reduce_sum.29
  28.3 2.4 %collective-permute-start.3 = (f32[8,256]{1,0:T(8,128)S(1)}, f32[8,256]{1,0:T(8,128)S(1)}, u32[]{:S(2)}, u32[]{:S(2)}) collective-permute-start(f32[8,256]{1,0:T(8,128)S(1)} %pad_maximum_fusion.1), channel_id=1, source_target_pairs={{0,8},{8,0},{16,24},{24,16},{32,40},{40,32},{48,56},{56,48},{64,72... | collective-permute-start | bytes 24584 | tf_op jit(solution)/shard_map/ppermute | solution.py:108
  31.0 0.1 copy.171
  31.1 0.1 reduce-window.33
  31.2 0.1 reduce.4
  31.3 0.6 reduce-window.31
  31.9 0.2 slice_reduce_fusion
  32.2 0.1 fusion.92
  32.3 0.1 multiply_add_fusion
  32.4 0.1 select_reduce_fusion.1
  32.5 0.3 compare_and_fusion.1
  32.8 0.4 fusion.28
  33.2 0.3 convolution_bitcast_fusion.14
  33.5 0.5 copy-done.2
  34.0 0.3 fusion.51
  34.3 0.3 convolution_bitcast_fusion.5
  34.6 0.3 convolution_bitcast_fusion.15
  34.9 0.4 fusion.32
  35.3 0.3 convolution_bitcast_fusion.12
  35.6 0.4 fusion.36
  36.0 0.3 fusion.63
  36.3 0.3 fusion.53
  36.6 0.3 fusion.62
  36.9 0.3 fusion.52
  37.2 0.2 convolution_select_fusion.1
  37.5 0.3 convolution_bitcast_fusion.13
  37.8 4.1 %collective-permute-start.7 = (bf16[256,256]{0,1:T(8,128)(2,1)S(1)}, bf16[256,256]{0,1:T(8,128)(2,1)S(1)}, u32[]{:S(2)}, u32[]{:S(2)}) collective-permute-start(bf16[256,256]{0,1:T(8,128)(2,1)S(1)} %pad_maximum_fusion), channel_id=1, source_target_pairs={{32,8},{48,24},{64,40},{80,56},{96,72},{112,88},{128,104},{144,120... | collective-permute-start | bytes 393224 | tf_op jit(solution)/shard_map/ppermute | solution.py:142
  41.9 0.4 fusion.44
  42.3 0.3 fusion.55
  42.6 0.3 fusion.56
  42.9 0.4 fusion.40
  43.2 0.3 convolution_bitcast_fusion.10
  43.6 0.3 fusion.54
  43.9 0.3 convolution_bitcast_fusion.11
  44.2 0.3 fusion.57
  44.4 1.9 %collective-permute-start.5 = (f32[256,1,4,128]{0,3,2,1:T(8,128)S(1)}, f32[256,1,4,128]{0,3,2,1:T(8,128)S(1)}, u32[]{:S(2)}, u32[]{:S(2)}) collective-permute-start(f32[256,1,4,128]{0,3,2,1:T(8,128)S(1)} %fusion.57), channel_id=1, source_target_pairs={{0,8},{8,0},{16,24},{24,16},{32,40},{40,32},{48,56},{56,48},{64,72... | collective-permute-start | bytes 1572872 | tf_op jit(solution)/shard_map/ppermute | solution.py:138
  46.4 9.4 %collective-permute-start.6 = (bf16[256,256]{0,1:T(8,128)(2,1)S(1)}, bf16[256,256]{0,1:T(8,128)(2,1)S(1)}, u32[]{:S(2)}, u32[]{:S(2)}) collective-permute-start(bf16[256,256]{0,1:T(8,128)(2,1)S(1)} %fusion.84), channel_id=1, source_target_pairs={{16,0},{24,8},{32,16},{40,24},{48,32},{56,40},{64,48},{72,56},{80,... | collective-permute-start | bytes 393224 | tf_op jit(solution)/shard_map/ppermute | solution.py:13
  55.8 0.3 convolution_bitcast_fusion.8
  56.1 0.3 convolution_bitcast_fusion.9
  56.4 12.3 %collective-permute-done.6 = bf16[256,256]{0,1:T(8,128)(2,1)S(1)} collective-permute-done((bf16[256,256]{0,1:T(8,128)(2,1)S(1)}, bf16[256,256]{0,1:T(8,128)(2,1)S(1)}, u32[]{:S(2)}, u32[]{:S(2)}) %collective-permute-start.6) | collective-permute-done | bytes 131104 | tf_op jit(solution)/shard_map/ppermute | solution.py:13
  68.8 0.3 fusion.61
  69.1 1.3 fusion.50
  70.4 15.7 %all-to-all-start = ((bf16[64,8,768]{2,1,0:T(8,128)(2,1)}), bf16[64,8,768]{2,1,0:T(8,128)(2,1)S(1)}, u32[]{:S(2)}, u32[]{:S(2)}) async-start(bf16[64,8,768]{2,1,0:T(8,128)(2,1)} %fusion.50), calls=%async_computation | async-start | bytes 1572864 | tf_op jit(solution)/shard_map/all_to_all | solution.py:173
  86.1 0.6 reduce-window.24
  86.8 0.2 slice_reduce_fusion.1
  87.2 1.2 select_reduce_fusion
  88.3 0.1 eq.94
  88.4 1.2 fusion.78
  89.6 0.1 and.98
  89.7 25.2 %all-to-all-done = bf16[64,8,768]{2,1,0:T(8,128)(2,1)S(1)} async-done(((bf16[64,8,768]{2,1,0:T(8,128)(2,1)}), bf16[64,8,768]{2,1,0:T(8,128)(2,1)S(1)}, u32[]{:S(2)}, u32[]{:S(2)}) %all-to-all-start) | async-done | bytes 786464 | tf_op jit(solution)/shard_map/all_to_all | solution.py:173
  114.9 0.4 convolution_convert_fusion.1
  115.3 37.0 %all_to_all.28 = bf16[8,32,768]{2,1,0:T(8,128)(2,1)S(1)} all-to-all(bf16[8,32,768]{2,1,0:T(8,128)(2,1)S(1)} %bitcast.409), channel_id=1, replica_groups=mesh['ctx'=64,'head'=8] {'head'}, dimensions={0} | all-to-all | bytes 786432 | tf_op jit(solution)/shard_map/all_to_all | solution.py:191
  152.3 0.7 copy.247
  153.1 0.6 copy.255
  153.7 0.6 copy.256
  (45 shorter events, 1.0 us)
Async XLA Ops:
  0.6 26.9 %copy-start = (bf16[256,512]{1,0:T(8,128)(2,1)S(1)}, bf16[256,512]{1,0:T(8,128)(2,1)}, u32[]{:S(2)}) copy-start(bf16[256,512]{1,0:T(8,128)(2,1)} %param.12) | copy-start | bytes 786436
  0.6 26.9 %copy-start.4 = (bf16[256,512]{1,0:T(8,128)(2,1)S(1)}, bf16[256,512]{1,0:T(8,128)(2,1)}, u32[]{:S(2)}) copy-start(bf16[256,512]{1,0:T(8,128)(2,1)} %param.11) | copy-start | bytes 786436
  2.4 33.2 %collective-permute-start.1 = (bf16[256,256]{1,0:T(8,128)(2,1)S(1)}, bf16[256,256]{1,0:T(8,128)(2,1)S(1)}, u32[]{:S(2)}, u32[]{:S(2)}) collective-permute-start(bf16[256,256]{1,0:T(8,128)(2,1)S(1)} %constant_dynamic-update-slice_fusion), channel_id=1, source_target_pairs={{8,32},{24,48},{40,64},{56,80},{72,96},{88,112},{104,128},{120,144... | collective-permute-start | bytes 393224 | tf_op jit(solution)/shard_map/ppermute | solution.py:80
  3.7 31.2 %collective-permute-start = (bf16[256,256]{1,0:T(8,128)(2,1)S(1)}, bf16[256,256]{1,0:T(8,128)(2,1)S(1)}, u32[]{:S(2)}, u32[]{:S(2)}) collective-permute-start(bf16[256,256]{1,0:T(8,128)(2,1)S(1)} %constant_dynamic-update-slice_fusion), channel_id=1, source_target_pairs={{0,16},{8,24},{16,32},{24,40},{32,48},{40,56},{48,64},{56,72},{64,... | collective-permute-start | bytes 393224 | tf_op jit(solution)/shard_map/ppermute | solution.py:13
  20.5 21.7 %collective-permute-start.4 = (bf16[256,512]{0,1:T(8,128)(2,1)S(1)}, bf16[256,512]{0,1:T(8,128)(2,1)S(1)}, u32[]{:S(2)}, u32[]{:S(2)}) collective-permute-start(bf16[256,512]{0,1:T(8,128)(2,1)S(1)} %copy.244), channel_id=1, source_target_pairs={{0,8},{8,0},{16,24},{24,16},{32,40},{40,32},{48,56},{56,48},{64,72... | collective-permute-start | bytes 786440 | tf_op jit(solution)/shard_map/ppermute | solution.py:107
  25.6 16.3 %collective-permute-start.2 = (bf16[256,512]{0,1:T(8,128)(2,1)S(1)}, bf16[256,512]{0,1:T(8,128)(2,1)S(1)}, u32[]{:S(2)}, u32[]{:S(2)}) collective-permute-start(bf16[256,512]{0,1:T(8,128)(2,1)S(1)} %copy.243), channel_id=1, source_target_pairs={{0,8},{8,0},{16,24},{24,16},{32,40},{40,32},{48,56},{56,48},{64,72... | collective-permute-start | bytes 786440 | tf_op jit(solution)/shard_map/ppermute | solution.py:106
  27.6 0.7 copy-start.5
  27.6 3.1 %copy-start.3 = (s32[16384]{0:T(1024)S(1)}, s32[16384]{0:T(1024)}, u32[]{:S(2)}) copy-start(s32[16384]{0:T(1024)} %param.15) | copy-start | bytes 196612
  27.6 3.3 %copy-start.6 = (s32[64]{0:T(128)S(1)}, s32[64]{0:T(128)}, u32[]{:S(2)}) copy-start(s32[64]{0:T(128)} %param.14) | copy-start | bytes 772
  27.8 5.0 %copy-start.1 = (bf16[256,128]{1,0:T(8,128)(2,1)S(1)}, bf16[256,128]{1,0:T(8,128)(2,1)}, u32[]{:S(2)}) copy-start(bf16[256,128]{1,0:T(8,128)(2,1)} %param.9) | copy-start | bytes 196612
  28.3 6.6 %collective-permute-start.3 = (f32[8,256]{1,0:T(8,128)S(1)}, f32[8,256]{1,0:T(8,128)S(1)}, u32[]{:S(2)}, u32[]{:S(2)}) collective-permute-start(f32[8,256]{1,0:T(8,128)S(1)} %pad_maximum_fusion.1), channel_id=1, source_target_pairs={{0,8},{8,0},{16,24},{24,16},{32,40},{40,32},{48,56},{56,48},{64,72... | collective-permute-start | bytes 24584 | tf_op jit(solution)/shard_map/ppermute | solution.py:108
  33.2 0.8 copy-start.2
  37.8 18.6 %collective-permute-start.7 = (bf16[256,256]{0,1:T(8,128)(2,1)S(1)}, bf16[256,256]{0,1:T(8,128)(2,1)S(1)}, u32[]{:S(2)}, u32[]{:S(2)}) collective-permute-start(bf16[256,256]{0,1:T(8,128)(2,1)S(1)} %pad_maximum_fusion), channel_id=1, source_target_pairs={{32,8},{48,24},{64,40},{80,56},{96,72},{112,88},{128,104},{144,120... | collective-permute-start | bytes 393224 | tf_op jit(solution)/shard_map/ppermute | solution.py:142
  44.4 24.4 %collective-permute-start.5 = (f32[256,1,4,128]{0,3,2,1:T(8,128)S(1)}, f32[256,1,4,128]{0,3,2,1:T(8,128)S(1)}, u32[]{:S(2)}, u32[]{:S(2)}) collective-permute-start(f32[256,1,4,128]{0,3,2,1:T(8,128)S(1)} %fusion.57), channel_id=1, source_target_pairs={{0,8},{8,0},{16,24},{24,16},{32,40},{40,32},{48,56},{56,48},{64,72... | collective-permute-start | bytes 1572872 | tf_op jit(solution)/shard_map/ppermute | solution.py:138
  46.4 22.3 %collective-permute-start.6 = (bf16[256,256]{0,1:T(8,128)(2,1)S(1)}, bf16[256,256]{0,1:T(8,128)(2,1)S(1)}, u32[]{:S(2)}, u32[]{:S(2)}) collective-permute-start(bf16[256,256]{0,1:T(8,128)(2,1)S(1)} %fusion.84), channel_id=1, source_target_pairs={{16,0},{24,8},{32,16},{40,24},{48,32},{56,40},{64,48},{72,56},{80,... | collective-permute-start | bytes 393224 | tf_op jit(solution)/shard_map/ppermute | solution.py:13
  70.4 44.5 %all-to-all-start = ((bf16[64,8,768]{2,1,0:T(8,128)(2,1)}), bf16[64,8,768]{2,1,0:T(8,128)(2,1)S(1)}, u32[]{:S(2)}, u32[]{:S(2)}) async-start(bf16[64,8,768]{2,1,0:T(8,128)(2,1)} %fusion.50), calls=%async_computation | async-start | bytes 1572864 | tf_op jit(solution)/shard_map/all_to_all | solution.py:173

commit v6 on v5

--- a/solution.py
+++ b/solution.py
@@ -103,8 +103,7 @@
         axis=3,
     )
     mine = query_side(block_index, query_head_rows, cotangent, logsumexp, row_correction)
-    their_q = lax.ppermute(query_head_rows, "ctx", partner)
-    their_do = lax.ppermute(cotangent, "ctx", partner)
+    their_low = lax.ppermute(jnp.concatenate([query_head_rows, cotangent], axis=1), "ctx", partner)
     their_high = lax.ppermute(
         jnp.concatenate([logsumexp, row_correction.reshape(length, -1).T], axis=0),
         "ctx",
@@ -112,8 +111,8 @@
     )
     theirs = query_side(
         block_index ^ 1,
-        their_q,
-        their_do,
+        their_low[:, :q_width],
+        their_low[:, q_width:],
         their_high[: logsumexp.shape[0]],
         their_high[logsumexp.shape[0] :].T.reshape(row_correction.shape),
     )
@@ -168,9 +167,15 @@
     pack = (
         lax.iota(jnp.int32, blocks * capacity)[:, None] == send_slots[None, :]
     ).astype(jnp.bfloat16)
-    packed = jnp.dot(pack, rows, preferred_element_type=jnp.float32).astype(jnp.bfloat16)
-
-    arrived = lax.all_to_all(packed, "ctx", split_axis=0, concat_axis=0, tiled=True)
+    packed_q = jnp.dot(pack, rows[:, :q_width], preferred_element_type=jnp.float32)
+    arrived_q = lax.all_to_all(
+        packed_q.astype(jnp.bfloat16), "ctx", split_axis=0, concat_axis=0, tiled=True
+    )
+    packed_kv = jnp.dot(pack, rows[:, q_width:], preferred_element_type=jnp.float32)
+    arrived_kv = lax.all_to_all(
+        packed_kv.astype(jnp.bfloat16), "ctx", split_axis=0, concat_axis=0, tiled=True
+    )
+    arrived = jnp.concatenate([arrived_q, arrived_kv], axis=1)
 
     all_owners = linear_row_index.reshape(blocks, length)
     landing = all_owners // length == block_index

time: 155 us -> 172 us (1.11)
  blocking collectives: 37 us -> 48.3 us
  waiting for transfers between devices: 37.5 us -> 43.4 us
  starting transfers between devices: 56.3 us -> 51.7 us
  other arithmetic: 5.38 us -> 7.82 us
    all_to_all x1, blocking collectives: 37 us -> 48.3 us  [per_device(): lax.all_to_all(linear_rows, 'head', split_axis=0, concat_axis=1, tiled=True)]
    ppermute x2, starting transfers between devices: 25.1 us -> 18.2 us  [from_behind(): return lax.ppermute(shard, axis, pairs)]
    all_to_all x1 -> x2, waiting for transfers between devices: 25.2 us -> 29.2 us  [the longest x1 16.7 us: per_device(): lax.all_to_all(packed_q.astype(jnp.bfloat16), 'ctx', split_axis=0, concat...]
    ppermute x2 -> x1, starting transfers between devices: 5.86 us -> 1.91 us  [per_device(): lax.ppermute(jnp.concatenate([query_head_rows, cotangent], axis=1), 'ctx'...]
    all_to_all x1 -> x2, starting transfers between devices: 15.7 us -> 19.6 us  [the longest x1 13.9 us: per_device(): lax.all_to_all(packed_kv.astype(jnp.bfloat16), 'ctx', split_axis=0, conca...]
    unnamed x17 -> x29, local copies, waits for them, and re-layouts: 1.53 us -> 3.7 us
    another operation x6, local copies, waits for them, and re-layouts: 2.46 us -> 0.56 us
  transfers between devices with their start and end apart: 9 -> 9, of which waited for: 2 -> 4; matrix products, arithmetic and copies ran while one was open for 10% -> 10% of each run, Pallas kernels for 0% -> 0%
where the time goes in v6:
time: 172 us; the launch traced here: 171 us
  starting transfers between devices  51.7 us (30%)
  blocking collectives  48.3 us (28%)
  waiting for transfers between devices  43.4 us (25%)
  matrix products  10.1 us (6%)
  local copies, waits for them, and re-layouts  8.49 us (5%)
  other arithmetic  7.82 us (5%)
    all_to_all x1, blocking collectives, per_device(): lax.all_to_all(linear_rows, 'head', split_axis=0, concat_axis=1, tiled=True)  48.3 us
    ppermute x2, starting transfers between devices, from_behind(): return lax.ppermute(shard, axis, pairs)  18.2 us
    all_to_all x1, waiting for transfers between devices, per_device(): lax.all_to_all(packed_q.astype(jnp.bfloat16), 'ctx', split_axis=0, concat...  16.7 us
    all_to_all x1, starting transfers between devices, per_device(): lax.all_to_all(packed_kv.astype(jnp.bfloat16), 'ctx', split_axis=0, conca...  13.9 us
    ppermute x2, waiting for transfers between devices, from_behind(): return lax.ppermute(shard, axis, pairs)  12.9 us
    all_to_all x1, waiting for transfers between devices, per_device(): lax.all_to_all(packed_kv.astype(jnp.bfloat16), 'ctx', split_axis=0, conca...  12.4 us
    all_to_all x1, starting transfers between devices, per_device(): lax.all_to_all(packed_q.astype(jnp.bfloat16), 'ctx', split_axis=0, concat...  5.73 us
    ppermute x1, starting transfers between devices, per_device(): lax.ppermute(kv_grad_three.astype(jnp.bfloat16), 'ctx', [(i, i - 3) for i...  4.58 us
  transfers between devices with their start and end apart: 9, of which 4 were waited for; matrix products, arithmetic and copies ran while one was open for 10% of the time, Pallas kernels for 0%

profile of v6, /device:TPU:2, one launch (start us, length us, event | category | flops | bytes accessed | tf_op | source)
XLA Modules:
  0.0 171.1 jit_solution(15674066531621286725)
XLA Ops:
  0.6 1.5 constant_dynamic-update-slice_fusion.1
  2.1 1.5 constant_dynamic-update-slice_fusion
  3.6 1.3 collective-permute-start.1
  4.9 15.7 %collective-permute-start = (bf16[256,256]{1,0:T(8,128)(2,1)}, bf16[256,256]{1,0:T(8,128)(2,1)S(1)}, u32[]{:S(2)}, u32[]{:S(2)}) collective-permute-start(bf16[256,256]{1,0:T(8,128)(2,1)} %constant_dynamic-update-slice_fusion), channel_id=1, source_target_pairs={{0,16},{8,24},{16,32},{24,40},{32,48},{40,56},{48,64},{56,72},{64,... | collective-permute-start | bytes 393224 | tf_op jit(solution)/shard_map/ppermute | solution.py:13
  20.6 1.1 convert_multiply_fusion
  21.7 0.2 mul.111
  21.9 0.3 reduce_sum.29
  22.4 4.1 %collective-permute-start.3 = (f32[8,256]{1,0:T(8,128)S(1)}, f32[8,256]{1,0:T(8,128)S(1)}, u32[]{:S(2)}, u32[]{:S(2)}) collective-permute-start(f32[8,256]{1,0:T(8,128)S(1)} %pad_maximum_fusion.2), channel_id=1, source_target_pairs={{0,8},{8,0},{16,24},{24,16},{32,40},{40,32},{48,56},{56,48},{64,72... | collective-permute-start | bytes 24584 | tf_op jit(solution)/shard_map/ppermute | solution.py:107
  26.5 0.1 copy.268
  26.7 0.1 copy.267
  26.8 0.8 pad_maximum_fusion
  27.6 1.9 %collective-permute-start.2 = (bf16[256,1024]{0,1:T(8,128)(2,1)}, bf16[256,1024]{0,1:T(8,128)(2,1)S(1)}, u32[]{:S(2)}, u32[]{:S(2)}) collective-permute-start(bf16[256,1024]{0,1:T(8,128)(2,1)} %pad_maximum_fusion), channel_id=1, source_target_pairs={{0,8},{8,0},{16,24},{24,16},{32,40},{40,32},{48,56},{56,48},{64,72... | collective-permute-start | bytes 1572872 | tf_op jit(solution)/shard_map/ppermute | solution.py:106
  30.2 0.6 reduce-window.31
  30.8 0.2 slice_reduce_fusion
  31.3 1.0 compare_and_fusion.1
  32.3 0.4 fusion.28
  32.6 0.3 convolution_bitcast_fusion.14
  33.0 0.5 copy-done.2
  33.5 0.3 fusion.51
  33.8 0.3 convolution_bitcast_fusion.15
  34.1 0.4 fusion.36
  34.5 0.3 fusion.64
  34.8 0.3 fusion.53
  35.1 0.3 fusion.63
  35.4 4.6 %collective-permute-start.6 = (bf16[256,256]{0,1:T(8,128)(2,1)S(1)}, bf16[256,256]{0,1:T(8,128)(2,1)S(1)}, u32[]{:S(2)}, u32[]{:S(2)}) collective-permute-start(bf16[256,256]{0,1:T(8,128)(2,1)S(1)} %pad_maximum_fusion.1), channel_id=1, source_target_pairs={{32,8},{48,24},{64,40},{80,56},{96,72},{112,88},{128,104},{144,120... | collective-permute-start | bytes 393224 | tf_op jit(solution)/shard_map/ppermute | solution.py:141
  40.1 0.4 fusion.32
  40.4 0.3 fusion.52
  40.7 0.3 convolution_bitcast_fusion.13
  41.0 0.3 convolution_bitcast_fusion.12
  41.4 0.5 copy-done.10
  41.9 0.4 fusion.44
  42.2 0.3 convolution_bitcast_fusion.8
  42.6 0.3 fusion.55
  42.9 0.5 copy-done.9
  43.4 0.4 fusion.40
  43.8 0.3 convolution_bitcast_fusion.10
  44.1 0.6 copy-done.4
  44.7 0.3 fusion.54
  45.0 0.3 convolution_bitcast_fusion.11
  45.3 2.5 %collective-permute-start.5 = (bf16[256,256]{0,1:T(8,128)(2,1)S(1)}, bf16[256,256]{0,1:T(8,128)(2,1)S(1)}, u32[]{:S(2)}, u32[]{:S(2)}) collective-permute-start(bf16[256,256]{0,1:T(8,128)(2,1)S(1)} %fusion.84), channel_id=1, source_target_pairs={{16,0},{24,8},{32,16},{40,24},{48,32},{56,40},{64,48},{72,56},{80,... | collective-permute-start | bytes 393224 | tf_op jit(solution)/shard_map/ppermute | solution.py:13
  47.8 0.3 fusion.56
  48.1 0.3 convolution_bitcast_fusion.9
  48.4 12.9 %collective-permute-done.5 = bf16[256,256]{0,1:T(8,128)(2,1)S(1)} collective-permute-done((bf16[256,256]{0,1:T(8,128)(2,1)S(1)}, bf16[256,256]{0,1:T(8,128)(2,1)S(1)}, u32[]{:S(2)}, u32[]{:S(2)}) %collective-permute-start.5) | collective-permute-done | bytes 131104 | tf_op jit(solution)/shard_map/ppermute | solution.py:13
  61.4 1.0 fusion.62
  62.4 13.9 %all-to-all-start.1 = ((bf16[64,8,256]{2,1,0:T(8,128)(2,1)}), bf16[64,8,256]{2,1,0:T(8,128)(2,1)S(1)}, u32[]{:S(2)}, u32[]{:S(2)}) async-start(bf16[64,8,256]{2,1,0:T(8,128)(2,1)} %fusion.62), calls=%async_computation.1 | async-start | bytes 524288 | tf_op jit(solution)/shard_map/all_to_all | solution.py:175
  76.3 0.3 fusion.57
  76.6 2.0 %collective-permute-start.4 = (f32[256,1,4,128]{0,3,2,1:T(8,128)S(1)}, f32[256,1,4,128]{0,3,2,1:T(8,128)S(1)}, u32[]{:S(2)}, u32[]{:S(2)}) collective-permute-start(f32[256,1,4,128]{0,3,2,1:T(8,128)S(1)} %fusion.57), channel_id=1, source_target_pairs={{0,8},{8,0},{16,24},{24,16},{32,40},{40,32},{48,56},{56,48},{64,72... | collective-permute-start | bytes 1572872 | tf_op jit(solution)/shard_map/ppermute | solution.py:137
  78.6 0.3 convolution_bitcast_fusion.5
  78.9 0.2 convolution_select_fusion.1
  79.1 1.2 collective-permute-done.4
  80.4 0.3 fusion.61
  80.6 1.1 fusion.50
  81.8 12.4 %all-to-all-done.1 = bf16[64,8,256]{2,1,0:T(8,128)(2,1)S(1)} async-done(((bf16[64,8,256]{2,1,0:T(8,128)(2,1)}), bf16[64,8,256]{2,1,0:T(8,128)(2,1)S(1)}, u32[]{:S(2)}, u32[]{:S(2)}) %all-to-all-start.1) | async-done | bytes 262176 | tf_op jit(solution)/shard_map/all_to_all | solution.py:175
  94.2 5.7 %all-to-all-start = ((bf16[64,8,512]{2,1,0:T(8,128)(2,1)}), bf16[64,8,512]{2,1,0:T(8,128)(2,1)S(1)}, u32[]{:S(2)}, u32[]{:S(2)}) async-start(bf16[64,8,512]{2,1,0:T(8,128)(2,1)} %fusion.50), calls=%async_computation | async-start | bytes 1048576 | tf_op jit(solution)/shard_map/all_to_all | solution.py:171
  100.0 0.6 reduce-window.24
  100.6 0.2 slice_reduce_fusion.1
  101.1 1.2 select_reduce_fusion
  102.3 1.2 fusion.81
  103.6 16.7 %all-to-all-done = bf16[64,8,512]{2,1,0:T(8,128)(2,1)S(1)} async-done(((bf16[64,8,512]{2,1,0:T(8,128)(2,1)}), bf16[64,8,512]{2,1,0:T(8,128)(2,1)S(1)}, u32[]{:S(2)}, u32[]{:S(2)}) %all-to-all-start) | async-done | bytes 524320 | tf_op jit(solution)/shard_map/all_to_all | solution.py:171
  120.3 0.4 convolution_convert_fusion.1
  120.7 48.3 %all_to_all.40 = bf16[8,32,768]{2,1,0:T(8,128)(2,1)S(1)} all-to-all(bf16[8,32,768]{2,1,0:T(8,128)(2,1)S(1)} %bitcast.436), channel_id=1, replica_groups=mesh['ctx'=64,'head'=8] {'head'}, dimensions={0} | all-to-all | bytes 786432 | tf_op jit(solution)/shard_map/all_to_all | solution.py:196
  169.1 0.7 copy.271
  169.8 0.6 copy.279
  170.5 0.6 copy.280
  (59 shorter events, 1.7 us)
Async XLA Ops:
  3.6 30.5 %collective-permute-start.1 = (bf16[256,256]{1,0:T(8,128)(2,1)}, bf16[256,256]{1,0:T(8,128)(2,1)S(1)}, u32[]{:S(2)}, u32[]{:S(2)}) collective-permute-start(bf16[256,256]{1,0:T(8,128)(2,1)} %constant_dynamic-update-slice_fusion), channel_id=1, source_target_pairs={{8,32},{24,48},{40,64},{56,80},{72,96},{88,112},{104,128},{120,144... | collective-permute-start | bytes 393224 | tf_op jit(solution)/shard_map/ppermute | solution.py:80
  4.9 35.2 %collective-permute-start = (bf16[256,256]{1,0:T(8,128)(2,1)}, bf16[256,256]{1,0:T(8,128)(2,1)S(1)}, u32[]{:S(2)}, u32[]{:S(2)}) collective-permute-start(bf16[256,256]{1,0:T(8,128)(2,1)} %constant_dynamic-update-slice_fusion), channel_id=1, source_target_pairs={{0,16},{8,24},{16,32},{24,40},{32,48},{40,56},{48,64},{56,72},{64,... | collective-permute-start | bytes 393224 | tf_op jit(solution)/shard_map/ppermute | solution.py:13
  21.7 0.7 copy-start.11
  21.7 4.8 %copy-start = (bf16[256,512]{1,0:T(8,128)(2,1)S(1)}, bf16[256,512]{1,0:T(8,128)(2,1)}, u32[]{:S(2)}) copy-start(bf16[256,512]{1,0:T(8,128)(2,1)} %param.12) | copy-start | bytes 786436
  21.7 4.9 %copy-start.6 = (bf16[256,512]{1,0:T(8,128)(2,1)S(1)}, bf16[256,512]{1,0:T(8,128)(2,1)}, u32[]{:S(2)}) copy-start(bf16[256,512]{1,0:T(8,128)(2,1)} %param.8) | copy-start | bytes 786436
  22.4 7.2 %copy-start.5 = (s32[16384]{0:T(1024)S(1)}, s32[16384]{0:T(1024)}, u32[]{:S(2)}) copy-start(s32[16384]{0:T(1024)} %param.15) | copy-start | bytes 196612
  22.4 7.4 %copy-start.12 = (s32[64]{0:T(128)S(1)}, s32[64]{0:T(128)}, u32[]{:S(2)}) copy-start(s32[64]{0:T(128)} %param.14) | copy-start | bytes 772
  22.4 11.7 %collective-permute-start.3 = (f32[8,256]{1,0:T(8,128)S(1)}, f32[8,256]{1,0:T(8,128)S(1)}, u32[]{:S(2)}, u32[]{:S(2)}) collective-permute-start(f32[8,256]{1,0:T(8,128)S(1)} %pad_maximum_fusion.2), channel_id=1, source_target_pairs={{0,8},{8,0},{16,24},{24,16},{32,40},{40,32},{48,56},{56,48},{64,72... | collective-permute-start | bytes 24584 | tf_op jit(solution)/shard_map/ppermute | solution.py:107
  26.8 5.5 %copy-start.1 = (bf16[256,128]{1,0:T(8,128)(2,1)S(1)}, bf16[256,128]{1,0:T(8,128)(2,1)}, u32[]{:S(2)}) copy-start(bf16[256,128]{1,0:T(8,128)(2,1)} %param.9) | copy-start | bytes 196612
  27.6 13.7 %collective-permute-start.2 = (bf16[256,1024]{0,1:T(8,128)(2,1)}, bf16[256,1024]{0,1:T(8,128)(2,1)S(1)}, u32[]{:S(2)}, u32[]{:S(2)}) collective-permute-start(bf16[256,1024]{0,1:T(8,128)(2,1)} %pad_maximum_fusion), channel_id=1, source_target_pairs={{0,8},{8,0},{16,24},{24,16},{32,40},{40,32},{48,56},{56,48},{64,72... | collective-permute-start | bytes 1572872 | tf_op jit(solution)/shard_map/ppermute | solution.py:106
  32.6 0.8 copy-start.2
  34.1 0.7 copy-start.7
  35.4 13.0 %collective-permute-start.6 = (bf16[256,256]{0,1:T(8,128)(2,1)S(1)}, bf16[256,256]{0,1:T(8,128)(2,1)S(1)}, u32[]{:S(2)}, u32[]{:S(2)}) collective-permute-start(bf16[256,256]{0,1:T(8,128)(2,1)S(1)} %pad_maximum_fusion.1), channel_id=1, source_target_pairs={{32,8},{48,24},{64,40},{80,56},{96,72},{112,88},{128,104},{144,120... | collective-permute-start | bytes 393224 | tf_op jit(solution)/shard_map/ppermute | solution.py:141
  40.0 2.8 %copy-start.3 = (bf16[256,256]{1,0:T(8,128)(2,1)}, bf16[256,256]{1,0:T(8,128)(2,1)S(1)}, u32[]{:S(2)}) copy-start(bf16[256,256]{1,0:T(8,128)(2,1)S(1)} %collective-permute-done) | copy-start | bytes 393220
  41.0 0.8 copy-start.10
  42.6 0.8 copy-start.9
  43.8 0.9 copy-start.4
  45.3 16.0 %collective-permute-start.5 = (bf16[256,256]{0,1:T(8,128)(2,1)S(1)}, bf16[256,256]{0,1:T(8,128)(2,1)S(1)}, u32[]{:S(2)}, u32[]{:S(2)}) collective-permute-start(bf16[256,256]{0,1:T(8,128)(2,1)S(1)} %fusion.84), channel_id=1, source_target_pairs={{16,0},{24,8},{32,16},{40,24},{48,32},{56,40},{64,48},{72,56},{80,... | collective-permute-start | bytes 393224 | tf_op jit(solution)/shard_map/ppermute | solution.py:13
  62.4 31.8 %all-to-all-start.1 = ((bf16[64,8,256]{2,1,0:T(8,128)(2,1)}), bf16[64,8,256]{2,1,0:T(8,128)(2,1)S(1)}, u32[]{:S(2)}, u32[]{:S(2)}) async-start(bf16[64,8,256]{2,1,0:T(8,128)(2,1)} %fusion.62), calls=%async_computation.1 | async-start | bytes 524288 | tf_op jit(solution)/shard_map/all_to_all | solution.py:175
  76.3 2.6 %copy-start.8 = (bf16[256,256]{1,0:T(8,128)(2,1)S(1)}, bf16[256,256]{1,0:T(8,128)(2,1)}, u32[]{:S(2)}) copy-start(bf16[256,256]{1,0:T(8,128)(2,1)} %copy-done.7) | copy-start | bytes 393220
  76.6 3.8 %collective-permute-start.4 = (f32[256,1,4,128]{0,3,2,1:T(8,128)S(1)}, f32[256,1,4,128]{0,3,2,1:T(8,128)S(1)}, u32[]{:S(2)}, u32[]{:S(2)}) collective-permute-start(f32[256,1,4,128]{0,3,2,1:T(8,128)S(1)} %fusion.57), channel_id=1, source_target_pairs={{0,8},{8,0},{16,24},{24,16},{32,40},{40,32},{48,56},{56,48},{64,72... | collective-permute-start | bytes 1572872 | tf_op jit(solution)/shard_map/ppermute | solution.py:137
  94.2 26.1 %all-to-all-start = ((bf16[64,8,512]{2,1,0:T(8,128)(2,1)}), bf16[64,8,512]{2,1,0:T(8,128)(2,1)S(1)}, u32[]{:S(2)}, u32[]{:S(2)}) async-start(bf16[64,8,512]{2,1,0:T(8,128)(2,1)} %fusion.50), calls=%async_computation | async-start | bytes 1048576 | tf_op jit(solution)/shard_map/all_to_all | solution.py:171

commit v7 on v5

--- a/solution.py
+++ b/solution.py
@@ -103,8 +103,7 @@
         axis=3,
     )
     mine = query_side(block_index, query_head_rows, cotangent, logsumexp, row_correction)
-    their_q = lax.ppermute(query_head_rows, "ctx", partner)
-    their_do = lax.ppermute(cotangent, "ctx", partner)
+    their_low = lax.ppermute(jnp.concatenate([query_head_rows, cotangent], axis=1), "ctx", partner)
     their_high = lax.ppermute(
         jnp.concatenate([logsumexp, row_correction.reshape(length, -1).T], axis=0),
         "ctx",
@@ -112,8 +111,8 @@
     )
     theirs = query_side(
         block_index ^ 1,
-        their_q,
-        their_do,
+        their_low[:, :q_width],
+        their_low[:, q_width:],
         their_high[: logsumexp.shape[0]],
         their_high[logsumexp.shape[0] :].T.reshape(row_correction.shape),
     )
@@ -135,7 +134,7 @@
     zero_q = jnp.zeros_like(q_own)
     zero_kv = jnp.zeros_like(kv_grad_own)
     sent_q = q_cross + jnp.where(even, q_next, zero_q)
-    back_q = lax.ppermute(sent_q, "ctx", partner)
+    back_q = lax.ppermute(sent_q.astype(jnp.bfloat16), "ctx", partner).astype(jnp.float32)
     query_acc = q_own + q_two + jnp.where(even, q_three, zero_q) + back_q
 
     crossed = from_behind((kv_grad_two + kv_grad_cross).astype(jnp.bfloat16), "ctx", -2)

time: 155 us -> 157 us (1.013)
  starting transfers between devices: 56.3 us -> 52.6 us
  waiting for transfers between devices: 37.5 us -> 41 us
  blocking collectives: 37 us -> 39.7 us
  local copies, waits for them, and re-layouts: 7.58 us -> 5.67 us
    ppermute x3 -> x2, starting transfers between devices: 7.78 us -> 3.84 us  [the longest x1 1.92 us: per_device(): lax.ppermute(jnp.concatenate([query_head_rows, cotangent], axis=1), 'ctx'...]
    all_to_all x1, blocking collectives: 37 us -> 39.7 us  [per_device(): lax.all_to_all(linear_rows, 'head', split_axis=0, concat_axis=1, tiled=True)]
    all_to_all x1, waiting for transfers between devices: 25.2 us -> 27.4 us  [per_device(): lax.all_to_all(packed, 'ctx', split_axis=0, concat_axis=0, tiled=True)]
    another operation x6, local copies, waits for them, and re-layouts: 2.46 us -> 0.56 us
    ppermute x1, starting transfers between devices: 2.4 us -> 4.07 us  [per_device(): lax.ppermute(jnp.concatenate([logsumexp, row_correction.reshape(length, -...]
  transfers between devices with their start and end apart: 9 -> 8, of which waited for: 2 -> 2; matrix products, arithmetic and copies ran while one was open for 10% -> 10% of each run, Pallas kernels for 0% -> 0%
where the time goes in v7:
time: 157 us; the launch traced here: 156 us
  starting transfers between devices  52.6 us (34%)
  waiting for transfers between devices  41 us (26%)
  blocking collectives  39.7 us (25%)
  matrix products  9.32 us (6%)
  other arithmetic  6.46 us (4%)
  local copies, waits for them, and re-layouts  5.67 us (4%)
    all_to_all x1, blocking collectives, per_device(): lax.all_to_all(linear_rows, 'head', split_axis=0, concat_axis=1, tiled=True)  39.7 us
    all_to_all x1, waiting for transfers between devices, per_device(): lax.all_to_all(packed, 'ctx', split_axis=0, concat_axis=0, tiled=True)  27.4 us
    ppermute x2, starting transfers between devices, from_behind(): return lax.ppermute(shard, axis, pairs)  24.1 us
    all_to_all x1, starting transfers between devices, per_device(): lax.all_to_all(packed, 'ctx', split_axis=0, concat_axis=0, tiled=True)  14.7 us
    ppermute x2, waiting for transfers between devices, from_behind(): return lax.ppermute(shard, axis, pairs)  13.6 us
    ppermute x1, starting transfers between devices, per_device(): lax.ppermute(kv_grad_three.astype(jnp.bfloat16), 'ctx', [(i, i - 3) for i...  4.57 us
    ppermute x1, starting transfers between devices, per_device(): lax.ppermute(jnp.concatenate([logsumexp, row_correction.reshape(length, -...  4.07 us
  transfers between devices with their start and end apart: 8, of which 2 were waited for; matrix products, arithmetic and copies ran while one was open for 10% of the time, Pallas kernels for 0%

profile of v7, /device:TPU:2, one launch (start us, length us, event | category | flops | bytes accessed | tf_op | source)
XLA Modules:
  0.0 156.0 jit_solution(15977898079234181923)
XLA Ops:
  0.6 0.9 constant_dynamic-update-slice_fusion.1
  1.5 0.9 constant_dynamic-update-slice_fusion
  2.3 1.3 collective-permute-start.1
  3.6 15.7 %collective-permute-start = (bf16[256,256]{1,0:T(8,128)(2,1)S(1)}, bf16[256,256]{1,0:T(8,128)(2,1)S(1)}, u32[]{:S(2)}, u32[]{:S(2)}) collective-permute-start(bf16[256,256]{1,0:T(8,128)(2,1)S(1)} %constant_dynamic-update-slice_fusion), channel_id=1, source_target_pairs={{0,16},{8,24},{16,32},{24,40},{32,48},{40,56},{48,64},{56,72},{64,... | collective-permute-start | bytes 393224 | tf_op jit(solution)/shard_map/ppermute | solution.py:13
  19.4 1.1 convert_multiply_fusion
  20.5 0.2 mul.111
  20.7 0.3 reduce_sum.29
  21.2 4.1 %collective-permute-start.3 = (f32[8,256]{1,0:T(8,128)S(1)}, f32[8,256]{1,0:T(8,128)S(1)}, u32[]{:S(2)}, u32[]{:S(2)}) collective-permute-start(f32[8,256]{1,0:T(8,128)S(1)} %pad_maximum_fusion.2), channel_id=1, source_target_pairs={{0,8},{8,0},{16,24},{24,16},{32,40},{40,32},{48,56},{56,48},{64,72... | collective-permute-start | bytes 24584 | tf_op jit(solution)/shard_map/ppermute | solution.py:107
  25.3 0.1 copy.268
  25.4 0.1 copy.267
  25.6 1.9 %collective-permute-start.2 = (bf16[256,1024]{0,1:T(8,128)(2,1)S(1)}, bf16[256,1024]{0,1:T(8,128)(2,1)S(1)}, u32[]{:S(2)}, u32[]{:S(2)}) collective-permute-start(bf16[256,1024]{0,1:T(8,128)(2,1)S(1)} %pad_maximum_fusion), channel_id=1, source_target_pairs={{0,8},{8,0},{16,24},{24,16},{32,40},{40,32},{48,56},{56,48},{64,72... | collective-permute-start | bytes 1572872 | tf_op jit(solution)/shard_map/ppermute | solution.py:106
  27.8 0.1 copy.191
  27.9 0.1 reduce-window.33
  28.0 0.1 reduce.4
  28.2 0.6 reduce-window.31
  28.8 0.2 slice_reduce_fusion
  29.0 0.1 fusion.93
  29.1 0.1 multiply_add_fusion
  29.2 0.1 select_reduce_fusion.1
  29.3 0.3 compare_and_fusion.1
  29.7 0.4 fusion.28
  30.0 0.3 convolution_bitcast_fusion.14
  30.4 0.5 copy-done.2
  30.9 0.3 fusion.51
  31.2 0.3 convolution_bitcast_fusion.5
  31.4 0.3 convolution_bitcast_fusion.15
  31.8 0.4 fusion.36
  32.2 0.3 fusion.64
  32.5 0.3 fusion.53
  32.8 0.3 fusion.63
  33.1 4.6 %collective-permute-start.6 = (bf16[256,256]{0,1:T(8,128)(2,1)S(1)}, bf16[256,256]{0,1:T(8,128)(2,1)S(1)}, u32[]{:S(2)}, u32[]{:S(2)}) collective-permute-start(bf16[256,256]{0,1:T(8,128)(2,1)S(1)} %pad_maximum_fusion.1), channel_id=1, source_target_pairs={{32,8},{48,24},{64,40},{80,56},{96,72},{112,88},{128,104},{144,120... | collective-permute-start | bytes 393224 | tf_op jit(solution)/shard_map/ppermute | solution.py:141
  37.7 0.4 fusion.32
  38.1 0.3 fusion.52
  38.4 0.3 convolution_bitcast_fusion.13
  38.7 0.3 convolution_bitcast_fusion.12
  39.0 0.2 convolution_select_fusion.1
  39.3 0.4 fusion.44
  39.7 0.3 convolution_bitcast_fusion.8
  40.0 0.3 fusion.55
  40.3 0.3 fusion.56
  40.6 0.4 fusion.40
  40.9 0.3 convolution_bitcast_fusion.10
  41.3 0.3 fusion.54
  41.5 0.3 convolution_bitcast_fusion.11
  41.9 0.3 fusion.62
  42.1 1.9 %collective-permute-start.4 = (bf16[256,1,4,128]{0,3,2,1:T(8,128)(2,1)S(1)}, bf16[256,1,4,128]{0,3,2,1:T(8,128)(2,1)S(1)}, u32[]{:S(2)}, u32[]{:S(2)}) collective-permute-start(bf16[256,1,4,128]{0,3,2,1:T(8,128)(2,1)S(1)} %fusion.62), channel_id=1, source_target_pairs={{0,8},{8,0},{16,24},{24,16},{32,40},{40,32},{48,56},{56,48},{64,72... | collective-permute-start | bytes 786440 | tf_op jit(solution)/shard_map/ppermute | solution.py:137
  44.1 8.3 %collective-permute-start.5 = (bf16[256,256]{0,1:T(8,128)(2,1)S(1)}, bf16[256,256]{0,1:T(8,128)(2,1)S(1)}, u32[]{:S(2)}, u32[]{:S(2)}) collective-permute-start(bf16[256,256]{0,1:T(8,128)(2,1)S(1)} %fusion.85), channel_id=1, source_target_pairs={{16,0},{24,8},{32,16},{40,24},{48,32},{56,40},{64,48},{72,56},{80,... | collective-permute-start | bytes 393224 | tf_op jit(solution)/shard_map/ppermute | solution.py:13
  52.4 0.3 convolution_bitcast_fusion.9
  52.8 13.6 %collective-permute-done.5 = bf16[256,256]{0,1:T(8,128)(2,1)S(1)} collective-permute-done((bf16[256,256]{0,1:T(8,128)(2,1)S(1)}, bf16[256,256]{0,1:T(8,128)(2,1)S(1)}, u32[]{:S(2)}, u32[]{:S(2)}) %collective-permute-start.5) | collective-permute-done | bytes 131104 | tf_op jit(solution)/shard_map/ppermute | solution.py:13
  66.4 0.3 fusion.60
  66.7 1.3 fusion.50
  68.0 14.7 %all-to-all-start = ((bf16[64,8,768]{2,1,0:T(8,128)(2,1)}), bf16[64,8,768]{2,1,0:T(8,128)(2,1)S(1)}, u32[]{:S(2)}, u32[]{:S(2)}) async-start(bf16[64,8,768]{2,1,0:T(8,128)(2,1)} %fusion.50), calls=%async_computation | async-start | bytes 1572864 | tf_op jit(solution)/shard_map/all_to_all | solution.py:172
  82.8 0.6 reduce-window.24
  83.5 0.2 slice_reduce_fusion.1
  83.9 1.2 select_reduce_fusion
  85.0 0.1 eq.94
  85.1 1.2 fusion.79
  86.3 0.1 and.98
  86.4 27.4 %all-to-all-done = bf16[64,8,768]{2,1,0:T(8,128)(2,1)S(1)} async-done(((bf16[64,8,768]{2,1,0:T(8,128)(2,1)}), bf16[64,8,768]{2,1,0:T(8,128)(2,1)S(1)}, u32[]{:S(2)}, u32[]{:S(2)}) %all-to-all-start) | async-done | bytes 786464 | tf_op jit(solution)/shard_map/all_to_all | solution.py:172
  113.8 0.4 convolution_convert_fusion.1
  114.2 39.7 %all_to_all.28 = bf16[8,32,768]{2,1,0:T(8,128)(2,1)S(1)} all-to-all(bf16[8,32,768]{2,1,0:T(8,128)(2,1)S(1)} %bitcast.433), channel_id=1, replica_groups=mesh['ctx'=64,'head'=8] {'head'}, dimensions={0} | all-to-all | bytes 786432 | tf_op jit(solution)/shard_map/all_to_all | solution.py:190
  154.0 0.7 copy.271
  154.7 0.6 copy.279
  155.3 0.6 copy.280
  (45 shorter events, 1.0 us)
Async XLA Ops:
  2.3 29.4 %collective-permute-start.1 = (bf16[256,256]{1,0:T(8,128)(2,1)S(1)}, bf16[256,256]{1,0:T(8,128)(2,1)S(1)}, u32[]{:S(2)}, u32[]{:S(2)}) collective-permute-start(bf16[256,256]{1,0:T(8,128)(2,1)S(1)} %constant_dynamic-update-slice_fusion), channel_id=1, source_target_pairs={{8,32},{24,48},{40,64},{56,80},{72,96},{88,112},{104,128},{120,144... | collective-permute-start | bytes 393224 | tf_op jit(solution)/shard_map/ppermute | solution.py:80
  3.6 34.0 %collective-permute-start = (bf16[256,256]{1,0:T(8,128)(2,1)S(1)}, bf16[256,256]{1,0:T(8,128)(2,1)S(1)}, u32[]{:S(2)}, u32[]{:S(2)}) collective-permute-start(bf16[256,256]{1,0:T(8,128)(2,1)S(1)} %constant_dynamic-update-slice_fusion), channel_id=1, source_target_pairs={{0,16},{8,24},{16,32},{24,40},{32,48},{40,56},{48,64},{56,72},{64,... | collective-permute-start | bytes 393224 | tf_op jit(solution)/shard_map/ppermute | solution.py:13
  20.5 0.7 copy-start.5
  20.5 4.8 %copy-start = (bf16[256,512]{1,0:T(8,128)(2,1)S(1)}, bf16[256,512]{1,0:T(8,128)(2,1)}, u32[]{:S(2)}) copy-start(bf16[256,512]{1,0:T(8,128)(2,1)} %param.12) | copy-start | bytes 786436
  20.5 4.9 %copy-start.4 = (bf16[256,512]{1,0:T(8,128)(2,1)S(1)}, bf16[256,512]{1,0:T(8,128)(2,1)}, u32[]{:S(2)}) copy-start(bf16[256,512]{1,0:T(8,128)(2,1)} %param.8) | copy-start | bytes 786436
  21.2 6.4 %copy-start.3 = (s32[16384]{0:T(1024)S(1)}, s32[16384]{0:T(1024)}, u32[]{:S(2)}) copy-start(s32[16384]{0:T(1024)} %param.15) | copy-start | bytes 196612
  21.2 6.6 %copy-start.6 = (s32[64]{0:T(128)S(1)}, s32[64]{0:T(128)}, u32[]{:S(2)}) copy-start(s32[64]{0:T(128)} %param.14) | copy-start | bytes 772
  21.2 10.6 %collective-permute-start.3 = (f32[8,256]{1,0:T(8,128)S(1)}, f32[8,256]{1,0:T(8,128)S(1)}, u32[]{:S(2)}, u32[]{:S(2)}) collective-permute-start(f32[8,256]{1,0:T(8,128)S(1)} %pad_maximum_fusion.2), channel_id=1, source_target_pairs={{0,8},{8,0},{16,24},{24,16},{32,40},{40,32},{48,56},{56,48},{64,72... | collective-permute-start | bytes 24584 | tf_op jit(solution)/shard_map/ppermute | solution.py:107
  25.6 4.1 %copy-start.1 = (bf16[256,128]{1,0:T(8,128)(2,1)S(1)}, bf16[256,128]{1,0:T(8,128)(2,1)}, u32[]{:S(2)}) copy-start(bf16[256,128]{1,0:T(8,128)(2,1)} %param.9) | copy-start | bytes 196612
  25.6 13.6 %collective-permute-start.2 = (bf16[256,1024]{0,1:T(8,128)(2,1)S(1)}, bf16[256,1024]{0,1:T(8,128)(2,1)S(1)}, u32[]{:S(2)}, u32[]{:S(2)}) collective-permute-start(bf16[256,1024]{0,1:T(8,128)(2,1)S(1)} %pad_maximum_fusion), channel_id=1, source_target_pairs={{0,8},{8,0},{16,24},{24,16},{32,40},{40,32},{48,56},{56,48},{64,72... | collective-permute-start | bytes 1572872 | tf_op jit(solution)/shard_map/ppermute | solution.py:106
  30.0 0.8 copy-start.2
  33.1 19.7 %collective-permute-start.6 = (bf16[256,256]{0,1:T(8,128)(2,1)S(1)}, bf16[256,256]{0,1:T(8,128)(2,1)S(1)}, u32[]{:S(2)}, u32[]{:S(2)}) collective-permute-start(bf16[256,256]{0,1:T(8,128)(2,1)S(1)} %pad_maximum_fusion.1), channel_id=1, source_target_pairs={{32,8},{48,24},{64,40},{80,56},{96,72},{112,88},{128,104},{144,120... | collective-permute-start | bytes 393224 | tf_op jit(solution)/shard_map/ppermute | solution.py:141
  42.1 24.3 %collective-permute-start.4 = (bf16[256,1,4,128]{0,3,2,1:T(8,128)(2,1)S(1)}, bf16[256,1,4,128]{0,3,2,1:T(8,128)(2,1)S(1)}, u32[]{:S(2)}, u32[]{:S(2)}) collective-permute-start(bf16[256,1,4,128]{0,3,2,1:T(8,128)(2,1)S(1)} %fusion.62), channel_id=1, source_target_pairs={{0,8},{8,0},{16,24},{24,16},{32,40},{40,32},{48,56},{56,48},{64,72... | collective-permute-start | bytes 786440 | tf_op jit(solution)/shard_map/ppermute | solution.py:137
  44.1 22.3 %collective-permute-start.5 = (bf16[256,256]{0,1:T(8,128)(2,1)S(1)}, bf16[256,256]{0,1:T(8,128)(2,1)S(1)}, u32[]{:S(2)}, u32[]{:S(2)}) collective-permute-start(bf16[256,256]{0,1:T(8,128)(2,1)S(1)} %fusion.85), channel_id=1, source_target_pairs={{16,0},{24,8},{32,16},{40,24},{48,32},{56,40},{64,48},{72,56},{80,... | collective-permute-start | bytes 393224 | tf_op jit(solution)/shard_map/ppermute | solution.py:13
  68.0 45.8 %all-to-all-start = ((bf16[64,8,768]{2,1,0:T(8,128)(2,1)}), bf16[64,8,768]{2,1,0:T(8,128)(2,1)S(1)}, u32[]{:S(2)}, u32[]{:S(2)}) async-start(bf16[64,8,768]{2,1,0:T(8,128)(2,1)} %fusion.50), calls=%async_computation | async-start | bytes 1572864 | tf_op jit(solution)/shard_map/all_to_all | solution.py:172
